TPU v7x, 256 devices: a whole 4x4x8 slice. The times are simulated.
256 devices in a mesh: row: 8 (over x_hi, y), feat: 32 (over x_lo, z, core).
Axes of the slice: x: 4 (x_hi: 2, x_lo: 2; x = x_hi * 2 + x_lo), y: 4, z: 8, core: 2. Of those that a mesh axis runs over, the one named last changes fastest.
Arguments:
- node_features: bfloat16 [1024, 65536], P('feat', 'row'), may hold values from -6 to 6
- adjacency: bfloat16 [2048, 128, 128], P('row'), may hold values from -0.5 to 0.5
- tile_row: int32 [2048], P('row'), may hold values from 0 to 63
- tile_col: int32 [2048], P('row'), may hold values from 0 to 63
- tile_count: int32 [8, 8], P('row'), may hold values from 1 to 32, as said below
- weight: bfloat16 [1024, 1024], P('feat'), may hold values from -0.1875 to 0.1875
- out_bias: float32 [1024], replicated, may hold values from -3 to 3
Outputs:
- activated: bfloat16 [1024, 65536], P('feat', 'row')
Inputs may be any that keep to these rules, and one draw needn't show every extreme that they name: tile_count[r, s] is at least 1; the entry with s equal to r is 32.
All inputs are finite; a program needn't handle non-finite values.
Results may differ from a plain program's by a relative error of at most 0.0095.
Values may be sent and summed in bfloat16 or wider, within the bound.
No kernel may reach another device: no remote copies, remote signals or barrier semaphores. Data moves between devices by JAX's collectives and lax.ppermute only.
A program may use at most 128 MiB of HBM per device.

v0:
```python
import jax
import jax.numpy as jnp
from jax import lax
from jax.sharding import PartitionSpec as P


def swap_with(value, axis, mask):
    count = lax.axis_size(axis)
    return lax.ppermute(value, axis, [(i, i ^ mask) for i in range(count)])


def weight_bits():
    bits = lax.axis_size("feat").bit_length() - 1
    return [bits - 1] + list(range(bits - 2, 0, -1)) + [0]


def gather_weight(held, bits):
    me = lax.axis_index("feat")
    for bit in bits:
        theirs = swap_with(held, "feat", 1 << bit)
        mine_low = ((me >> bit) & 1) == 0
        low = jnp.where(mine_low, held, theirs)
        high = jnp.where(mine_low, theirs, held)
        held = jnp.stack([low, high], axis=1).reshape(-1, *held.shape[1:])
    return held


def on_device(node_features, adjacency, tile_row, tile_col, tile_count, weight, out_bias):
    feat_width = node_features.shape[0]
    rows_here = node_features.shape[1]
    tile_size = adjacency.shape[1]
    row_blocks = rows_here // tile_size
    cycle_len = lax.axis_size("row")
    slot_total = tile_row.shape[0] // cycle_len
    own_row = lax.axis_index("row")
    counts_here = tile_count[0]

    bits = weight_bits()
    w_mid = gather_weight(weight.reshape(1, *weight.shape), bits[:3])
    cols_out = lax.all_to_all(tile_col.reshape(cycle_len, slot_total), "row", 0, 0, tiled=True)
    w_mid, cols_out = lax.optimization_barrier((w_mid, cols_out))
    blocks_t = node_features.reshape(feat_width, row_blocks, tile_size).transpose(1, 0, 2)

    tile_ids = jnp.arange(cycle_len * slot_total)
    live_all = (tile_ids % slot_total) < counts_here[tile_ids // slot_total]
    onehot_all = (
        (tile_row[:, None] == jnp.arange(row_blocks)[None, :]) & live_all[:, None]
    ).astype(jnp.float32).reshape(cycle_len, slot_total, row_blocks)

    def add_source(running, picked, source):
        tiles_part = lax.dynamic_slice_in_dim(adjacency, source * slot_total, slot_total, 0)
        onehot = lax.dynamic_index_in_dim(onehot_all, source, 0, keepdims=False)
        product = jnp.einsum("sfj,sji->fsi", picked, tiles_part, preferred_element_type=jnp.float32)
        return running + jnp.einsum("fsi,sr->fri", product, onehot)

    dests = jnp.bitwise_xor(own_row, jnp.arange(1, cycle_len))
    send_cols = jnp.take(cols_out, dests, axis=0).reshape(-1)
    picked_all = jnp.take(blocks_t, send_cols, axis=0).reshape(
        cycle_len - 1, slot_total, feat_width, tile_size
    )
    held = [swap_with(picked_all[m - 1], "row", m) for m in range(1, cycle_len)]
    own_cols = lax.dynamic_slice_in_dim(tile_col, own_row * slot_total, slot_total, 0)
    running = jnp.zeros((feat_width, row_blocks, tile_size), jnp.float32)
    running = add_source(running, jnp.take(blocks_t, own_cols, axis=0), own_row)
    for step_num in range(1, cycle_len):
        running = add_source(running, held[step_num - 1], jnp.bitwise_xor(own_row, step_num))
    w_mid, _ = lax.optimization_barrier((gather_weight(w_mid, bits[3:4]), running))
    w_full = gather_weight(w_mid, bits[4:]).reshape(-1, weight.shape[1])
    aggregated = running.reshape(feat_width, rows_here).astype(jnp.bfloat16)
    agg_t = lax.all_to_all(aggregated, "feat", 1, 0, tiled=True)
    pre_act = jnp.dot(w_full, agg_t, preferred_element_type=jnp.float32)
    act_t = jax.nn.relu(pre_act + out_bias[:, None]).astype(jnp.bfloat16)
    activated = lax.all_to_all(act_t, "feat", 0, 1, tiled=True)
    return activated


def solution(mesh):
    in_specs = (
        P("feat", "row"),
        P("row", None, None),
        P("row"),
        P("row"),
        P("row", None),
        P("feat", None),
        P(),
    )
    out_specs = P("feat", "row")

    return jax.shard_map(on_device, mesh=mesh, in_specs=in_specs, out_specs=out_specs, check_vma=False)
```

profile of v0, /device:TPU:1, one launch (start us, length us, event | category | flops | bytes accessed | tf_op | source)
XLA Modules:
  0.0 130.5 jit_solution(10454954550698003874)
XLA Ops:
  0.0 2.0 %collective-permute-start = (bf16[1,32,1024]{2,1,0:T(8,128)(2,1)}, bf16[1,32,1024]{2,1,0:T(8,128)(2,1)S(1)}, u32[]{:S(2)}, u32[]{:S(2)}) collective-permute-start(bf16[1,32,1024]{2,1,0:T(8,128)(2,1)} %bitcast.133), channel_id=1, source_target_pairs={{0,16},{1,17},{2,18},{3,19},{4,20},{5,21},{6,22},{7,23},{8,24},{9,... | collective-permute-start | bytes 196616 | tf_op jit(solution)/shard_map/ppermute | solution.py:9
  3.4 6.4 %all-to-all-start = ((s32[8,1,32]{2,1,0:T(1,128)}), s32[8,1,32]{2,1,0:T(1,128)S(1)}, u32[]{:S(2)}, u32[]{:S(2)}) async-start(s32[8,1,32]{2,1,0:T(1,128)} %all_to_all.34), calls=%async_computation | async-start | bytes 8192 | tf_op jit(solution)/shard_map/all_to_all | solution.py:40
  9.9 1.6 %fusion.63 = (s32[1,1]{1,0:T(1,128)}, s32[1,1]{1,0:T(1,128)}, s32[1,1]{1,0:T(1,128)}, s32[1,1]{1,0:T(1,128)}, s32[1,1]{1,0:T(1,128)}, /*index=5*/s32[1,1]{1,0:T(1,128)}, s32[1,1]{1,0:T(1,128)}, s32[1,1]{1,0:T(1,128)}) fusion(s32[1,8]{1,0:T(1,128)} %param.11), kind=kLoop, calls=%fused_computation.127 | loop fusion | bytes 64 | tf_op jit(solution)/shard_map/gather | solution.py:45
  11.5 4.5 %compare_select_fusion.2 = s32[256,1]{0,1:T(1,128)S(1)} fusion(s32[]{:T(128)} %bitcast.16, s32[]{:T(128)} %bitcast.17, s32[]{:T(128)} %bitcast.18, s32[]{:T(128)} %bitcast.19, s32[]{:T(128)} %bitcast.20, s32[]{:T(128)} %bitcast.22, s32[]{:T(128)} %bitcast.21), kind=kLoop, calls=%fused_computation.105 | loop fusion | flops 5888 | bytes 1052 | tf_op jit(solution)/shard_map/gather | solution.py:45
  17.7 7.0 %collective-permute-start.1 = (bf16[2,32,1024]{2,1,0:T(8,128)(2,1)S(1)}, bf16[2,32,1024]{2,1,0:T(8,128)(2,1)S(1)}, u32[]{:S(2)}, u32[]{:S(2)}) collective-permute-start(bf16[2,32,1024]{2,1,0:T(8,128)(2,1)S(1)} %maximum_bitcast_fusion), channel_id=1, source_target_pairs={{0,8},{1,9},{2,10},{3,11},{4,12},{5,13},{6,14},{7,15},{8,0},{9,1},... | collective-permute-start | bytes 393224 | tf_op jit(solution)/shard_map/ppermute | solution.py:9
  25.4 1.7 %collective-permute-done.1 = bf16[2,32,1024]{2,1,0:T(8,128)(2,1)S(1)} collective-permute-done((bf16[2,32,1024]{2,1,0:T(8,128)(2,1)S(1)}, bf16[2,32,1024]{2,1,0:T(8,128)(2,1)S(1)}, u32[]{:S(2)}, u32[]{:S(2)}) %collective-permute-start.1) | collective-permute-done | bytes 131104 | tf_op jit(solution)/shard_map/ppermute | solution.py:9
  27.2 5.2 %collective-permute-start.2 = (bf16[4,32,1024]{2,1,0:T(8,128)(2,1)S(1)}, bf16[4,32,1024]{2,1,0:T(8,128)(2,1)S(1)}, u32[]{:S(2)}, u32[]{:S(2)}) collective-permute-start(bf16[4,32,1024]{2,1,0:T(8,128)(2,1)S(1)} %bitcast.129), channel_id=1, source_target_pairs={{0,4},{1,5},{2,6},{3,7},{4,0},{5,1},{6,2},{7,3},{8,12},{9,13},{10,... | collective-permute-start | bytes 786440 | tf_op jit(solution)/shard_map/ppermute | solution.py:9
  33.8 2.4 %convolution_bitcast_fusion.7 = bf16[32,32,128]{2,0,1:T(8,128)(2,1)} fusion(bf16[256,128,128]{2,1,0:T(8,128)(2,1)} %param.8, s32[]{:T(128)S(6)} %select_n.225, bf16[32,32,128]{2,1,0:T(8,128)(2,1)S(1)} %gather_fusion, pred[32]{0:T(512)(128)(4,1)S(1)} %get-tuple-element.11), kind=kOutput, calls=%fused_computation.23 | convolution fusion | flops 33685504 | bytes 1572900 | tf_op jit(solution)/shard_map/sfj,sji->fsi/dot_general | solution.py:53
  36.2 6.9 %collective-permute-done.2 = bf16[4,32,1024]{2,1,0:T(8,128)(2,1)S(1)} collective-permute-done((bf16[4,32,1024]{2,1,0:T(8,128)(2,1)S(1)}, bf16[4,32,1024]{2,1,0:T(8,128)(2,1)S(1)}, u32[]{:S(2)}, u32[]{:S(2)}) %collective-permute-start.2) | collective-permute-done | bytes 262176 | tf_op jit(solution)/shard_map/ppermute | solution.py:9
  48.7 2.5 %collective-permute-start.5 = (bf16[32,32,128]{2,1,0:T(8,128)(2,1)S(1)}, bf16[32,32,128]{2,1,0:T(8,128)(2,1)S(1)}, u32[]{:S(2)}, u32[]{:S(2)}) collective-permute-start(bf16[32,32,128]{2,1,0:T(8,128)(2,1)S(1)} %get-tuple-element.20), channel_id=1, source_target_pairs={{0,64},{32,96},{64,0},{96,32},{128,192},{160,224},{192,128},{224,1... | collective-permute-start | bytes 786440 | tf_op jit(solution)/shard_map/ppermute | solution.py:9
  51.3 2.9 %collective-permute-start.7 = (bf16[32,32,128]{2,1,0:T(8,128)(2,1)S(1)}, bf16[32,32,128]{2,1,0:T(8,128)(2,1)S(1)}, u32[]{:S(2)}, u32[]{:S(2)}) collective-permute-start(bf16[32,32,128]{2,1,0:T(8,128)(2,1)S(1)} %get-tuple-element.18), channel_id=1, source_target_pairs={{0,128},{32,160},{64,192},{96,224},{128,0},{160,32},{192,64},{224,... | collective-permute-start | bytes 786440 | tf_op jit(solution)/shard_map/ppermute | solution.py:9
  54.2 6.0 %collective-permute-start.9 = (bf16[32,32,128]{2,1,0:T(8,128)(2,1)S(1)}, bf16[32,32,128]{2,1,0:T(8,128)(2,1)S(1)}, u32[]{:S(2)}, u32[]{:S(2)}) collective-permute-start(bf16[32,32,128]{2,1,0:T(8,128)(2,1)S(1)} %get-tuple-element.16), channel_id=1, source_target_pairs={{0,192},{32,224},{64,128},{96,160},{128,64},{160,96},{192,0},{224,... | collective-permute-start | bytes 786440 | tf_op jit(solution)/shard_map/ppermute | solution.py:9
  60.1 1.6 %convolution_bitcast_fusion.6 = bf16[32,32,128]{2,0,1:T(8,128)(2,1)S(1)} fusion(bf16[32,32,128]{2,1,0:T(8,128)(2,1)S(1)} %collective-permute-done.4, bf16[256,128,128]{2,1,0:T(8,128)(2,1)} %param.8, s32[]{:T(128)S(6)} %select_n.229), kind=kOutput, calls=%fused_computation.22 | convolution fusion | flops 33554432 | bytes 1572868 | tf_op jit(solution)/shard_map/sfj,sji->fsi/dot_general | solution.py:53
  63.6 1.6 %convolution_bitcast_fusion.5 = bf16[32,32,128]{2,0,1:T(8,128)(2,1)S(1)} fusion(bf16[32,32,128]{2,1,0:T(8,128)(2,1)S(1)} %collective-permute-done.5, bf16[256,128,128]{2,1,0:T(8,128)(2,1)} %param.8, s32[]{:T(128)S(6)} %select_n.239), kind=kOutput, calls=%fused_computation.21 | convolution fusion | flops 33554432 | bytes 1572868 | tf_op jit(solution)/shard_map/sfj,sji->fsi/dot_general | solution.py:53
  65.9 1.6 %convolution_bitcast_fusion.4 = bf16[32,32,128]{2,0,1:T(8,128)(2,1)S(1)} fusion(bf16[32,32,128]{2,1,0:T(8,128)(2,1)S(1)} %collective-permute-done.6, bf16[256,128,128]{2,1,0:T(8,128)(2,1)} %param.8, s32[]{:T(128)S(6)} %select_n.241), kind=kOutput, calls=%fused_computation.20 | convolution fusion | flops 33554432 | bytes 1572868 | tf_op jit(solution)/shard_map/sfj,sji->fsi/dot_general | solution.py:53
  67.9 1.6 %convolution_bitcast_fusion.3 = bf16[32,32,128]{2,0,1:T(8,128)(2,1)S(1)} fusion(bf16[32,32,128]{2,1,0:T(8,128)(2,1)S(1)} %collective-permute-done.7, bf16[256,128,128]{2,1,0:T(8,128)(2,1)} %param.8, s32[]{:T(128)S(6)} %select_n.243), kind=kOutput, calls=%fused_computation.19 | convolution fusion | flops 33554432 | bytes 1572868 | tf_op jit(solution)/shard_map/sfj,sji->fsi/dot_general | solution.py:53
  69.9 1.6 %convolution_bitcast_fusion.2 = bf16[32,32,128]{2,0,1:T(8,128)(2,1)S(1)} fusion(bf16[32,32,128]{2,1,0:T(8,128)(2,1)S(1)} %collective-permute-done.8, bf16[256,128,128]{2,1,0:T(8,128)(2,1)} %param.8, s32[]{:T(128)S(6)} %select_n.245), kind=kOutput, calls=%fused_computation.18 | convolution fusion | flops 33554432 | bytes 1572868 | tf_op jit(solution)/shard_map/sfj,sji->fsi/dot_general | solution.py:53
  72.6 1.6 %convolution_bitcast_fusion.1 = bf16[32,32,128]{2,0,1:T(8,128)(2,1)S(1)} fusion(bf16[32,32,128]{2,1,0:T(8,128)(2,1)S(1)} %collective-permute-done.9, bf16[256,128,128]{2,1,0:T(8,128)(2,1)} %param.8, s32[]{:T(128)S(6)} %select_n.247), kind=kOutput, calls=%fused_computation.17 | convolution fusion | flops 33554432 | bytes 1572868 | tf_op jit(solution)/shard_map/sfj,sji->fsi/dot_general | solution.py:53
  74.5 3.7 %collective-permute-done.10 = bf16[32,32,128]{2,1,0:T(8,128)(2,1)S(1)} collective-permute-done((bf16[32,32,128]{2,1,0:T(8,128)(2,1)S(1)}, bf16[32,32,128]{2,1,0:T(8,128)(2,1)S(1)}, u32[]{:S(2)}, u32[]{:S(2)}) %collective-permute-start.10) | collective-permute-done | bytes 262176 | tf_op jit(solution)/shard_map/ppermute | solution.py:9
  78.3 1.6 %convolution_bitcast_fusion = bf16[32,32,128]{2,0,1:T(8,128)(2,1)S(1)} fusion(bf16[32,32,128]{2,1,0:T(8,128)(2,1)S(1)} %collective-permute-done.10, bf16[256,128,128]{2,1,0:T(8,128)(2,1)} %param.8, s32[]{:T(128)S(6)} %select_n.249), kind=kOutput, calls=%fused_computation.16 | convolution fusion | flops 33554432 | bytes 1572868 | tf_op jit(solution)/shard_map/sfj,sji->fsi/dot_general | solution.py:53
  80.6 2.5 %collective-permute-start.11 = (bf16[16,32,1024]{2,1,0:T(8,128)(2,1)S(1)}, bf16[16,32,1024]{2,1,0:T(8,128)(2,1)}, u32[]{:S(2)}, u32[]{:S(2)}) collective-permute-start(bf16[16,32,1024]{2,1,0:T(8,128)(2,1)S(1)} %bitcast.123), channel_id=1, source_target_pairs={{0,1},{1,0},{2,3},{3,2},{4,5},{5,4},{6,7},{7,6},{8,9},{9,8},{10,11... | collective-permute-start | bytes 3145736 | tf_op jit(solution)/shard_map/ppermute | solution.py:9
  84.3 6.6 %all-to-all-start.1 = ((bf16[32,32,256]{2,0,1:T(8,128)(2,1)}), bf16[32,32,256]{2,0,1:T(8,128)(2,1)S(1)}, u32[]{:S(2)}, u32[]{:S(2)}) async-start(bf16[32,32,256]{2,0,1:T(8,128)(2,1)} %copy.58), calls=%async_computation.1 | async-start | bytes 1048576 | tf_op jit(solution)/shard_map/all_to_all | solution.py:70
  92.7 14.8 %all-to-all-done.1 = bf16[32,32,256]{2,0,1:T(8,128)(2,1)S(1)} async-done(((bf16[32,32,256]{2,0,1:T(8,128)(2,1)}), bf16[32,32,256]{2,0,1:T(8,128)(2,1)S(1)}, u32[]{:S(2)}, u32[]{:S(2)}) %all-to-all-start.1) | async-done | bytes 524320 | tf_op jit(solution)/shard_map/all_to_all | solution.py:70
  108.2 21.4 %all_to_all.47 = bf16[32,32,256]{2,1,0:T(8,128)(2,1)S(1)} all-to-all(bf16[32,32,256]{2,1,0:T(8,128)(2,1)S(1)} %bitcast.131), channel_id=1, replica_groups=mesh['row'=8,'feat'=32] {'feat'}, dimensions={0} | all-to-all | bytes 1048576 | tf_op jit(solution)/shard_map/all_to_all | solution.py:73
  (68 shorter events, 20.8 us)
Async XLA Ops:
  0.0 9.8 %copy-start = (bf16[32,8192]{1,0:T(8,128)(2,1)S(1)}, bf16[32,8192]{1,0:T(8,128)(2,1)}, u32[]{:S(2)}) copy-start(bf16[32,8192]{1,0:T(8,128)(2,1)} %param.7) | copy-start | bytes 1572868
  0.0 16.8 %collective-permute-start = (bf16[1,32,1024]{2,1,0:T(8,128)(2,1)}, bf16[1,32,1024]{2,1,0:T(8,128)(2,1)S(1)}, u32[]{:S(2)}, u32[]{:S(2)}) collective-permute-start(bf16[1,32,1024]{2,1,0:T(8,128)(2,1)} %bitcast.133), channel_id=1, source_target_pairs={{0,16},{1,17},{2,18},{3,19},{4,20},{5,21},{6,22},{7,23},{8,24},{9,... | collective-permute-start | bytes 196616 | tf_op jit(solution)/shard_map/ppermute | solution.py:9
  3.4 39.8 %all-to-all-start = ((s32[8,1,32]{2,1,0:T(1,128)}), s32[8,1,32]{2,1,0:T(1,128)S(1)}, u32[]{:S(2)}, u32[]{:S(2)}) async-start(s32[8,1,32]{2,1,0:T(1,128)} %all_to_all.34), calls=%async_computation | async-start | bytes 8192 | tf_op jit(solution)/shard_map/all_to_all | solution.py:40
  17.7 9.5 %collective-permute-start.1 = (bf16[2,32,1024]{2,1,0:T(8,128)(2,1)S(1)}, bf16[2,32,1024]{2,1,0:T(8,128)(2,1)S(1)}, u32[]{:S(2)}, u32[]{:S(2)}) collective-permute-start(bf16[2,32,1024]{2,1,0:T(8,128)(2,1)S(1)} %maximum_bitcast_fusion), channel_id=1, source_target_pairs={{0,8},{1,9},{2,10},{3,11},{4,12},{5,13},{6,14},{7,15},{8,0},{9,1},... | collective-permute-start | bytes 393224 | tf_op jit(solution)/shard_map/ppermute | solution.py:9
  27.2 15.8 %collective-permute-start.2 = (bf16[4,32,1024]{2,1,0:T(8,128)(2,1)S(1)}, bf16[4,32,1024]{2,1,0:T(8,128)(2,1)S(1)}, u32[]{:S(2)}, u32[]{:S(2)}) collective-permute-start(bf16[4,32,1024]{2,1,0:T(8,128)(2,1)S(1)} %bitcast.129), channel_id=1, source_target_pairs={{0,4},{1,5},{2,6},{3,7},{4,0},{5,1},{6,2},{7,3},{8,12},{9,13},{10,... | collective-permute-start | bytes 786440 | tf_op jit(solution)/shard_map/ppermute | solution.py:9
  45.7 8.4 %collective-permute-start.4 = (bf16[32,32,128]{2,1,0:T(8,128)(2,1)S(1)}, bf16[32,32,128]{2,1,0:T(8,128)(2,1)S(1)}, u32[]{:S(2)}, u32[]{:S(2)}) collective-permute-start(bf16[32,32,128]{2,1,0:T(8,128)(2,1)S(1)} %get-tuple-element.21), channel_id=1, source_target_pairs={{0,32},{32,0},{64,96},{96,64},{128,160},{160,128},{192,224},{224,1... | collective-permute-start | bytes 786440 | tf_op jit(solution)/shard_map/ppermute | solution.py:9
  48.7 13.4 %collective-permute-start.5 = (bf16[32,32,128]{2,1,0:T(8,128)(2,1)S(1)}, bf16[32,32,128]{2,1,0:T(8,128)(2,1)S(1)}, u32[]{:S(2)}, u32[]{:S(2)}) collective-permute-start(bf16[32,32,128]{2,1,0:T(8,128)(2,1)S(1)} %get-tuple-element.20), channel_id=1, source_target_pairs={{0,64},{32,96},{64,0},{96,32},{128,192},{160,224},{192,128},{224,1... | collective-permute-start | bytes 786440 | tf_op jit(solution)/shard_map/ppermute | solution.py:9
  51.2 14.4 %collective-permute-start.6 = (bf16[32,32,128]{2,1,0:T(8,128)(2,1)S(1)}, bf16[32,32,128]{2,1,0:T(8,128)(2,1)S(1)}, u32[]{:S(2)}, u32[]{:S(2)}) collective-permute-start(bf16[32,32,128]{2,1,0:T(8,128)(2,1)S(1)} %get-tuple-element.19), channel_id=1, source_target_pairs={{0,96},{32,64},{64,32},{96,0},{128,224},{160,192},{192,160},{224,1... | collective-permute-start | bytes 786440 | tf_op jit(solution)/shard_map/ppermute | solution.py:9
  51.3 16.6 %collective-permute-start.7 = (bf16[32,32,128]{2,1,0:T(8,128)(2,1)S(1)}, bf16[32,32,128]{2,1,0:T(8,128)(2,1)S(1)}, u32[]{:S(2)}, u32[]{:S(2)}) collective-permute-start(bf16[32,32,128]{2,1,0:T(8,128)(2,1)S(1)} %get-tuple-element.18), channel_id=1, source_target_pairs={{0,128},{32,160},{64,192},{96,224},{128,0},{160,32},{192,64},{224,... | collective-permute-start | bytes 786440 | tf_op jit(solution)/shard_map/ppermute | solution.py:9
  54.1 15.7 %collective-permute-start.8 = (bf16[32,32,128]{2,1,0:T(8,128)(2,1)S(1)}, bf16[32,32,128]{2,1,0:T(8,128)(2,1)S(1)}, u32[]{:S(2)}, u32[]{:S(2)}) collective-permute-start(bf16[32,32,128]{2,1,0:T(8,128)(2,1)S(1)} %get-tuple-element.17), channel_id=1, source_target_pairs={{0,160},{32,128},{64,224},{96,192},{128,32},{160,0},{192,96},{224,... | collective-permute-start | bytes 786440 | tf_op jit(solution)/shard_map/ppermute | solution.py:9
  54.2 18.4 %collective-permute-start.9 = (bf16[32,32,128]{2,1,0:T(8,128)(2,1)S(1)}, bf16[32,32,128]{2,1,0:T(8,128)(2,1)S(1)}, u32[]{:S(2)}, u32[]{:S(2)}) collective-permute-start(bf16[32,32,128]{2,1,0:T(8,128)(2,1)S(1)} %get-tuple-element.16), channel_id=1, source_target_pairs={{0,192},{32,224},{64,128},{96,160},{128,64},{160,96},{192,0},{224,... | collective-permute-start | bytes 786440 | tf_op jit(solution)/shard_map/ppermute | solution.py:9
  62.1 16.1 %collective-permute-start.10 = (bf16[32,32,128]{2,1,0:T(8,128)(2,1)S(1)}, bf16[32,32,128]{2,1,0:T(8,128)(2,1)S(1)}, u32[]{:S(2)}, u32[]{:S(2)}) collective-permute-start(bf16[32,32,128]{2,1,0:T(8,128)(2,1)S(1)} %get-tuple-element.15), channel_id=1, source_target_pairs={{0,224},{32,192},{64,160},{96,128},{128,96},{160,64},{192,32},{224... | collective-permute-start | bytes 786440 | tf_op jit(solution)/shard_map/ppermute | solution.py:9
  65.6 14.6 %collective-permute-start.3 = (bf16[8,32,1024]{2,1,0:T(8,128)(2,1)S(1)}, bf16[8,32,1024]{2,1,0:T(8,128)(2,1)S(1)}, u32[]{:S(2)}, u32[]{:S(2)}) collective-permute-start(bf16[8,32,1024]{2,1,0:T(8,128)(2,1)S(1)} %bitcast.125), channel_id=1, source_target_pairs={{0,2},{1,3},{2,0},{3,1},{4,6},{5,7},{6,4},{7,5},{8,10},{9,11},{10,... | collective-permute-start | bytes 1572872 | tf_op jit(solution)/shard_map/ppermute | solution.py:9
  80.5 27.0 %copy-start.1 = (f32[1024]{0:T(1024)S(1)}, f32[1024]{0:T(1024)}, u32[]{:S(2)}) copy-start(f32[1024]{0:T(1024)} %param.13) | copy-start | bytes 12292
  80.6 10.4 %collective-permute-start.11 = (bf16[16,32,1024]{2,1,0:T(8,128)(2,1)S(1)}, bf16[16,32,1024]{2,1,0:T(8,128)(2,1)}, u32[]{:S(2)}, u32[]{:S(2)}) collective-permute-start(bf16[16,32,1024]{2,1,0:T(8,128)(2,1)S(1)} %bitcast.123), channel_id=1, source_target_pairs={{0,1},{1,0},{2,3},{3,2},{4,5},{5,4},{6,7},{7,6},{8,9},{9,8},{10,11... | collective-permute-start | bytes 3145736 | tf_op jit(solution)/shard_map/ppermute | solution.py:9
  84.3 23.2 %all-to-all-start.1 = ((bf16[32,32,256]{2,0,1:T(8,128)(2,1)}), bf16[32,32,256]{2,0,1:T(8,128)(2,1)S(1)}, u32[]{:S(2)}, u32[]{:S(2)}) async-start(bf16[32,32,256]{2,0,1:T(8,128)(2,1)} %copy.58), calls=%async_computation.1 | async-start | bytes 1048576 | tf_op jit(solution)/shard_map/all_to_all | solution.py:70
where the time goes:
time: 132 us; the launch traced here: 130 us
  starting transfers between devices  44.4 us (34%)
  waiting for transfers between devices  27.8 us (21%)
  blocking collectives  21.4 us (16%)
  matrix products  18.2 us (14%)
  other arithmetic  9.27 us (7%)
  local copies, waits for them, and re-layouts  8.96 us (7%)
    ppermute x12, starting transfers between devices, swap_with(): return lax.ppermute(value, axis, [(i, i ^ mask) for i in range(count)])  31.4 us
    all_to_all x1, blocking collectives, on_device(): activated = lax.all_to_all(act_t, 'feat', 0, 1, tiled=True)  21.4 us
    all_to_all x1, waiting for transfers between devices, on_device(): agg_t = lax.all_to_all(aggregated, 'feat', 1, 0, tiled=True)  14.8 us
    dot_general x8, matrix products, add_source(): jnp.einsum('sfj,sji->fsi', picked, tiles_part, preferred_element_type=jnp...  13.6 us
    ppermute x12, waiting for transfers between devices, swap_with(): return lax.ppermute(value, axis, [(i, i ^ mask) for i in range(count)])  13 us
    all_to_all x1, starting transfers between devices, on_device(): agg_t = lax.all_to_all(aggregated, 'feat', 1, 0, tiled=True)  6.64 us
    all_to_all x1, starting transfers between devices, on_device(): lax.all_to_all(tile_col.reshape(cycle_len, slot_total), 'row', 0, 0, tile...  6.36 us
    gather x3, other arithmetic, on_device(): live_all = tile_ids % slot_total < counts_here[tile_ids // slot_total]  5.18 us
  transfers between devices with their start and end apart: 14, of which 5 were waited for; matrix products, arithmetic and copies ran while one was open for 24% of the time, Pallas kernels for 0%

commit v1 on v0

--- a/solution.py
+++ b/solution.py
@@ -9,20 +9,19 @@
     return lax.ppermute(value, axis, [(i, i ^ mask) for i in range(count)])
 
 
-def weight_bits():
-    bits = lax.axis_size("feat").bit_length() - 1
-    return [bits - 1] + list(range(bits - 2, 0, -1)) + [0]
-
-
-def gather_weight(held, bits):
+def gather_weight(weight):
+    feat_count = lax.axis_size("feat")
     me = lax.axis_index("feat")
-    for bit in bits:
+    bits = feat_count.bit_length() - 1
+    order = [bits - 1] + list(range(bits - 2, 0, -1)) + [0]
+    held = weight.reshape(1, -1, weight.shape[1])
+    for bit in order:
         theirs = swap_with(held, "feat", 1 << bit)
         mine_low = ((me >> bit) & 1) == 0
         low = jnp.where(mine_low, held, theirs)
         high = jnp.where(mine_low, theirs, held)
         held = jnp.stack([low, high], axis=1).reshape(-1, *held.shape[1:])
-    return held
+    return held.reshape(-1, weight.shape[1])
 
 
 def on_device(node_features, adjacency, tile_row, tile_col, tile_count, weight, out_bias):
@@ -35,10 +34,8 @@
     own_row = lax.axis_index("row")
     counts_here = tile_count[0]
 
-    bits = weight_bits()
-    w_mid = gather_weight(weight.reshape(1, *weight.shape), bits[:3])
+    w_full = gather_weight(weight)
     cols_out = lax.all_to_all(tile_col.reshape(cycle_len, slot_total), "row", 0, 0, tiled=True)
-    w_mid, cols_out = lax.optimization_barrier((w_mid, cols_out))
     blocks_t = node_features.reshape(feat_width, row_blocks, tile_size).transpose(1, 0, 2)
 
     tile_ids = jnp.arange(cycle_len * slot_total)
@@ -53,19 +50,28 @@
         product = jnp.einsum("sfj,sji->fsi", picked, tiles_part, preferred_element_type=jnp.float32)
         return running + jnp.einsum("fsi,sr->fri", product, onehot)
 
-    dests = jnp.bitwise_xor(own_row, jnp.arange(1, cycle_len))
+    whole = (1, 3)
+    picked_m = [m for m in range(1, cycle_len) if m not in whole]
+    dests = jnp.bitwise_xor(own_row, jnp.array(picked_m))
     send_cols = jnp.take(cols_out, dests, axis=0).reshape(-1)
     picked_all = jnp.take(blocks_t, send_cols, axis=0).reshape(
-        cycle_len - 1, slot_total, feat_width, tile_size
+        len(picked_m), slot_total, feat_width, tile_size
     )
-    held = [swap_with(picked_all[m - 1], "row", m) for m in range(1, cycle_len)]
-    own_cols = lax.dynamic_slice_in_dim(tile_col, own_row * slot_total, slot_total, 0)
+
+    def own_cols_of(source):
+        return lax.dynamic_slice_in_dim(tile_col, source * slot_total, slot_total, 0)
+
+    held = {}
+    for m in whole:
+        block = swap_with(node_features, "row", m)
+        block_t = block.reshape(feat_width, row_blocks, tile_size).transpose(1, 0, 2)
+        held[m] = jnp.take(block_t, own_cols_of(jnp.bitwise_xor(own_row, m)), axis=0)
+    for i, m in enumerate(picked_m):
+        held[m] = swap_with(picked_all[i], "row", m)
     running = jnp.zeros((feat_width, row_blocks, tile_size), jnp.float32)
-    running = add_source(running, jnp.take(blocks_t, own_cols, axis=0), own_row)
+    running = add_source(running, jnp.take(blocks_t, own_cols_of(own_row), axis=0), own_row)
     for step_num in range(1, cycle_len):
-        running = add_source(running, held[step_num - 1], jnp.bitwise_xor(own_row, step_num))
-    w_mid, _ = lax.optimization_barrier((gather_weight(w_mid, bits[3:4]), running))
-    w_full = gather_weight(w_mid, bits[4:]).reshape(-1, weight.shape[1])
+        running = add_source(running, held[step_num], jnp.bitwise_xor(own_row, step_num))
     aggregated = running.reshape(feat_width, rows_here).astype(jnp.bfloat16)
     agg_t = lax.all_to_all(aggregated, "feat", 1, 0, tiled=True)
     pre_act = jnp.dot(w_full, agg_t, preferred_element_type=jnp.float32)

time: 132 us -> 130 us (0.985)
  starting transfers between devices: 44.4 us -> 39 us
  local copies, waits for them, and re-layouts: 8.96 us -> 13.2 us
  matrix products: 18.2 us -> 15 us
  waiting for transfers between devices: 27.8 us -> 31 us
    dot_general x8, matrix products: 13.6 us -> 9.52 us  [add_source(): jnp.einsum('sfj,sji->fsi', picked, tiles_part, preferred_element_type=jnp...]
    all_to_all x1, starting transfers between devices: 6.64 us -> 4.2 us  [on_device(): agg_t = lax.all_to_all(aggregated, 'feat', 1, 0, tiled=True)]
    transpose x0 -> x2, local copies, waits for them, and re-layouts: none -> 2.27 us  [on_device(): block.reshape(feat_width, row_blocks, tile_size).transpose(1, 0, 2)]
    ppermute x12, waiting for transfers between devices: 13 us -> 15.1 us  [swap_with(): return lax.ppermute(value, axis, [(i, i ^ mask) for i in range(count)])]
    ppermute x12, starting transfers between devices: 31.4 us -> 29.6 us  [swap_with(): return lax.ppermute(value, axis, [(i, i ^ mask) for i in range(count)])]
  transfers between devices with their start and end apart: 14 -> 14, of which waited for: 5 -> 6; matrix products, arithmetic and copies ran while one was open for 24% -> 25% of each run, Pallas kernels for 0% -> 0%
where the time goes in v1:
time: 130 us; the launch traced here: 129 us
  starting transfers between devices  39 us (30%)
  waiting for transfers between devices  31 us (24%)
  blocking collectives  21.4 us (16%)
  matrix products  15 us (12%)
  local copies, waits for them, and re-layouts  13.2 us (10%)
  other arithmetic  8.74 us (7%)
    ppermute x12, starting transfers between devices, swap_with(): return lax.ppermute(value, axis, [(i, i ^ mask) for i in range(count)])  29.6 us
    all_to_all x1, blocking collectives, on_device(): activated = lax.all_to_all(act_t, 'feat', 0, 1, tiled=True)  21.4 us
    all_to_all x1, waiting for transfers between devices, on_device(): agg_t = lax.all_to_all(aggregated, 'feat', 1, 0, tiled=True)  16 us
    ppermute x12, waiting for transfers between devices, swap_with(): return lax.ppermute(value, axis, [(i, i ^ mask) for i in range(count)])  15.1 us
    dot_general x8, matrix products, add_source(): jnp.einsum('sfj,sji->fsi', picked, tiles_part, preferred_element_type=jnp...  9.52 us
    all_to_all x1, starting transfers between devices, on_device(): lax.all_to_all(tile_col.reshape(cycle_len, slot_total), 'row', 0, 0, tile...  5.2 us
    gather x3, other arithmetic, on_device(): live_all = tile_ids % slot_total < counts_here[tile_ids // slot_total]  4.9 us
    dot_general x8, matrix products, add_source(): return running + jnp.einsum('fsi,sr->fri', product, onehot)  4.77 us
  transfers between devices with their start and end apart: 14, of which 6 were waited for; matrix products, arithmetic and copies ran while one was open for 25% of the time, Pallas kernels for 0%

profile of v1, /device:TPU:1, one launch (start us, length us, event | category | flops | bytes accessed | tf_op | source)
XLA Modules:
  0.0 128.8 jit_solution(8122319236875447389)
XLA Ops:
  0.0 3.6 %collective-permute-start.7 = (bf16[32,8192]{1,0:T(8,128)(2,1)}, bf16[32,8192]{1,0:T(8,128)(2,1)}, u32[]{:S(2)}, u32[]{:S(2)}) collective-permute-start(bf16[32,8192]{1,0:T(8,128)(2,1)} %param.10), channel_id=1, source_target_pairs={{0,96},{32,64},{64,32},{96,0},{128,224},{160,192},{192,160},{224,1... | collective-permute-start | bytes 1572872 | tf_op jit(solution)/shard_map/ppermute | solution.py:9
  3.6 1.4 %all_to_all.34 = s32[8,1,32]{2,1,0:T(1,128)} reshape(s32[256]{0:T(256)} %param.13) | data formatting | bytes 2048 | tf_op jit(solution)/shard_map/all_to_all | solution.py:38
  4.9 5.2 %all-to-all-start = ((s32[8,1,32]{2,1,0:T(1,128)}), s32[8,1,32]{2,1,0:T(1,128)S(1)}, u32[]{:S(2)}, u32[]{:S(2)}) async-start(s32[8,1,32]{2,1,0:T(1,128)} %all_to_all.34), calls=%async_computation | async-start | bytes 8192 | tf_op jit(solution)/shard_map/all_to_all | solution.py:38
  13.9 1.6 %fusion.71 = (s32[1,1]{1,0:T(1,128)}, s32[1,1]{1,0:T(1,128)}, s32[1,1]{1,0:T(1,128)}, s32[1,1]{1,0:T(1,128)}, s32[1,1]{1,0:T(1,128)}, /*index=5*/s32[1,1]{1,0:T(1,128)}, s32[1,1]{1,0:T(1,128)}, s32[1,1]{1,0:T(1,128)}) fusion(s32[1,8]{1,0:T(1,128)} %param.14), kind=kLoop, calls=%fused_computation.144 | loop fusion | bytes 64 | tf_op jit(solution)/shard_map/gather | solution.py:42
  15.6 4.2 %compare_select_fusion.2 = s32[256,1]{0,1:T(1,128)S(1)} fusion(s32[]{:T(128)} %bitcast.18, s32[]{:T(128)} %bitcast.19, s32[]{:T(128)} %bitcast.20, s32[]{:T(128)} %bitcast.21, s32[]{:T(128)} %bitcast.22, s32[]{:T(128)} %bitcast.24, s32[]{:T(128)} %bitcast.23), kind=kLoop, calls=%fused_computation.118 | loop fusion | flops 5888 | bytes 1052 | tf_op jit(solution)/shard_map/gather | solution.py:42
  21.3 1.7 %convolution_bitcast_fusion.7 = bf16[32,32,128]{2,0,1:T(8,128)(2,1)S(1)} fusion(bf16[256,128,128]{2,1,0:T(8,128)(2,1)} %param.11, s32[]{:T(128)S(6)} %select_n.216, bf16[32,32,128]{2,1,0:T(8,128)(2,1)S(1)} %gather_fusion.2, pred[32]{0:T(512)(128)(4,1)S(1)} %get-tuple-element.31), kind=kOutput, calls=%fused_computation.26 | convolution fusion | flops 33685504 | bytes 1572900 | tf_op jit(solution)/shard_map/sfj,sji->fsi/dot_general | solution.py:50
  25.4 7.0 %collective-permute-start.1 = (bf16[2,32,1024]{2,1,0:T(8,128)(2,1)S(1)}, bf16[2,32,1024]{2,1,0:T(8,128)(2,1)S(1)}, u32[]{:S(2)}, u32[]{:S(2)}) collective-permute-start(bf16[2,32,1024]{2,1,0:T(8,128)(2,1)S(1)} %maximum_bitcast_fusion), channel_id=1, source_target_pairs={{0,8},{1,9},{2,10},{3,11},{4,12},{5,13},{6,14},{7,15},{8,0},{9,1},... | collective-permute-start | bytes 393224 | tf_op jit(solution)/shard_map/ppermute | solution.py:9
  32.6 5.8 %collective-permute-start.11 = (bf16[32,32,128]{2,1,0:T(8,128)(2,1)S(1)}, bf16[32,32,128]{2,1,0:T(8,128)(2,1)S(1)}, u32[]{:S(2)}, u32[]{:S(2)}) collective-permute-start(bf16[32,32,128]{2,1,0:T(8,128)(2,1)S(1)} %get-tuple-element.16), channel_id=1, source_target_pairs={{0,224},{32,192},{64,160},{96,128},{128,96},{160,64},{192,32},{224... | collective-permute-start | bytes 786440 | tf_op jit(solution)/shard_map/ppermute | solution.py:9
  38.8 2.9 %collective-permute-start.9 = (bf16[32,32,128]{2,1,0:T(8,128)(2,1)S(1)}, bf16[32,32,128]{2,1,0:T(8,128)(2,1)S(1)}, u32[]{:S(2)}, u32[]{:S(2)}) collective-permute-start(bf16[32,32,128]{2,1,0:T(8,128)(2,1)S(1)} %get-tuple-element.18), channel_id=1, source_target_pairs={{0,160},{32,128},{64,224},{96,192},{128,32},{160,0},{192,96},{224,... | collective-permute-start | bytes 786440 | tf_op jit(solution)/shard_map/ppermute | solution.py:9
  42.7 2.4 %collective-permute-start.8 = (bf16[32,32,128]{2,1,0:T(8,128)(2,1)S(1)}, bf16[32,32,128]{2,1,0:T(8,128)(2,1)S(1)}, u32[]{:S(2)}, u32[]{:S(2)}) collective-permute-start(bf16[32,32,128]{2,1,0:T(8,128)(2,1)S(1)} %get-tuple-element.19), channel_id=1, source_target_pairs={{0,128},{32,160},{64,192},{96,224},{128,0},{160,32},{192,64},{224,... | collective-permute-start | bytes 786440 | tf_op jit(solution)/shard_map/ppermute | solution.py:9
  45.1 1.6 %convolution_bitcast_fusion = bf16[32,32,128]{2,0,1:T(8,128)(2,1)S(1)} fusion(bf16[32,32,128]{2,1,0:T(8,128)(2,1)S(1)} %collective-permute-done.11, bf16[256,128,128]{2,1,0:T(8,128)(2,1)} %param.11, s32[]{:T(128)S(6)} %select_n.237), kind=kOutput, calls=%fused_computation.19 | convolution fusion | flops 33554432 | bytes 1572868 | tf_op jit(solution)/shard_map/sfj,sji->fsi/dot_general | solution.py:50
  46.7 1.9 %collective-permute-done.10 = bf16[32,32,128]{2,1,0:T(8,128)(2,1)S(1)} collective-permute-done((bf16[32,32,128]{2,1,0:T(8,128)(2,1)S(1)}, bf16[32,32,128]{2,1,0:T(8,128)(2,1)S(1)}, u32[]{:S(2)}, u32[]{:S(2)}) %collective-permute-start.10) | collective-permute-done | bytes 262176 | tf_op jit(solution)/shard_map/ppermute | solution.py:9
  48.6 2.6 %collective-permute-start.6 = (bf16[32,32,128]{2,1,0:T(8,128)(2,1)S(1)}, bf16[32,32,128]{2,1,0:T(8,128)(2,1)S(1)}, u32[]{:S(2)}, u32[]{:S(2)}) collective-permute-start(bf16[32,32,128]{2,1,0:T(8,128)(2,1)S(1)} %get-tuple-element.20), channel_id=1, source_target_pairs={{0,64},{32,96},{64,0},{96,32},{128,192},{160,224},{192,128},{224,1... | collective-permute-start | bytes 786440 | tf_op jit(solution)/shard_map/ppermute | solution.py:9
  51.6 2.7 %collective-permute-done.9 = bf16[32,32,128]{2,1,0:T(8,128)(2,1)S(1)} collective-permute-done((bf16[32,32,128]{2,1,0:T(8,128)(2,1)S(1)}, bf16[32,32,128]{2,1,0:T(8,128)(2,1)S(1)}, u32[]{:S(2)}, u32[]{:S(2)}) %collective-permute-start.9) | collective-permute-done | bytes 262176 | tf_op jit(solution)/shard_map/ppermute | solution.py:9
  55.9 3.9 %collective-permute-done.8 = bf16[32,32,128]{2,1,0:T(8,128)(2,1)S(1)} collective-permute-done((bf16[32,32,128]{2,1,0:T(8,128)(2,1)S(1)}, bf16[32,32,128]{2,1,0:T(8,128)(2,1)S(1)}, u32[]{:S(2)}, u32[]{:S(2)}) %collective-permute-start.8) | collective-permute-done | bytes 262176 | tf_op jit(solution)/shard_map/ppermute | solution.py:9
  61.3 5.5 %collective-permute-done.2 = bf16[4,32,1024]{2,1,0:T(8,128)(2,1)S(1)} collective-permute-done((bf16[4,32,1024]{2,1,0:T(8,128)(2,1)S(1)}, bf16[4,32,1024]{2,1,0:T(8,128)(2,1)S(1)}, u32[]{:S(2)}, u32[]{:S(2)}) %collective-permute-start.2) | collective-permute-done | bytes 262176 | tf_op jit(solution)/shard_map/ppermute | solution.py:9
  69.0 2.4 %convolution_bitcast_fusion.4 = bf16[32,32,128]{2,0,1:T(8,128)(2,1)} fusion(bf16[256,128,128]{2,1,0:T(8,128)(2,1)} %param.11, s32[]{:T(128)S(6)} %select_n.229, bf16[32,32,128]{2,1,0:T(8,128)(2,1)S(1)} %gather_fusion.4, pred[32]{0:T(512)(128)(4,1)S(1)} %get-tuple-element.6), kind=kOutput, calls=%fused_computation.23 | convolution fusion | flops 33685504 | bytes 1572900 | tf_op jit(solution)/shard_map/sfj,sji->fsi/dot_general | solution.py:50
  73.1 1.7 %convolution_bitcast_fusion.6 = bf16[32,32,128]{2,0,1:T(8,128)(2,1)S(1)} fusion(bf16[256,128,128]{2,1,0:T(8,128)(2,1)} %param.11, s32[]{:T(128)S(6)} %select_n.218, bf16[32,32,128]{2,1,0:T(8,128)(2,1)S(1)} %gather_fusion.3, pred[32]{0:T(512)(128)(4,1)S(1)} %get-tuple-element.29), kind=kOutput, calls=%fused_computation.25 | convolution fusion | flops 33685504 | bytes 1572900 | tf_op jit(solution)/shard_map/sfj,sji->fsi/dot_general | solution.py:50
  75.2 1.3 %convolution_add_fusion.5 = f32[64,32,128]{2,0,1:T(8,128)S(1)} fusion(f32[64,32,128]{2,0,1:T(8,128)S(1)} %convolution_add_fusion.6, bf16[32,32,128]{2,0,1:T(8,128)(2,1)} %convolution_bitcast_fusion.5, pred[8,32,64]{2,1,0:T(32,128)(4,1)S(1)} %fusion.30, s32[]{:T(128)S(6)} %select_n.219), kind=kOutput, calls=%fused_computation.11 | convolution fusion | flops 17039360 | bytes 2363396 | tf_op jit(solution)/shard_map/fsi,sr->fri/dot_general | solution.py:51
  76.5 1.3 %convolution_add_fusion.4 = f32[64,32,128]{2,0,1:T(8,128)S(1)} fusion(f32[64,32,128]{2,0,1:T(8,128)S(1)} %convolution_add_fusion.5, bf16[32,32,128]{2,0,1:T(8,128)(2,1)} %convolution_bitcast_fusion.4, pred[8,32,64]{2,1,0:T(32,128)(4,1)S(1)} %fusion.30, s32[]{:T(128)S(6)} %select_n.228), kind=kOutput, calls=%fused_computation.10 | convolution fusion | flops 17039360 | bytes 2363396 | tf_op jit(solution)/shard_map/fsi,sr->fri/dot_general | solution.py:51
  79.8 3.2 %collective-permute-start.4 = (bf16[16,32,1024]{2,1,0:T(8,128)(2,1)S(1)}, bf16[16,32,1024]{2,1,0:T(8,128)(2,1)S(1)}, u32[]{:S(2)}, u32[]{:S(2)}) collective-permute-start(bf16[16,32,1024]{2,1,0:T(8,128)(2,1)S(1)} %bitcast.137), channel_id=1, source_target_pairs={{0,1},{1,0},{2,3},{3,2},{4,5},{5,4},{6,7},{7,6},{8,9},{9,8},{10,11... | collective-permute-start | bytes 3145736 | tf_op jit(solution)/shard_map/ppermute | solution.py:9
  85.1 4.2 %all-to-all-start.1 = ((bf16[32,32,256]{2,0,1:T(8,128)(2,1)}), bf16[32,32,256]{2,0,1:T(8,128)(2,1)S(1)}, u32[]{:S(2)}, u32[]{:S(2)}) async-start(bf16[32,32,256]{2,0,1:T(8,128)(2,1)} %copy.65), calls=%async_computation.1 | async-start | bytes 1048576 | tf_op jit(solution)/shard_map/all_to_all | solution.py:76
  89.9 16.0 %all-to-all-done.1 = bf16[32,32,256]{2,0,1:T(8,128)(2,1)S(1)} async-done(((bf16[32,32,256]{2,0,1:T(8,128)(2,1)}), bf16[32,32,256]{2,0,1:T(8,128)(2,1)S(1)}, u32[]{:S(2)}, u32[]{:S(2)}) %all-to-all-start.1) | async-done | bytes 524320 | tf_op jit(solution)/shard_map/all_to_all | solution.py:76
  106.6 21.4 %all_to_all.47 = bf16[32,32,256]{2,1,0:T(8,128)(2,1)S(1)} all-to-all(bf16[32,32,256]{2,1,0:T(8,128)(2,1)S(1)} %bitcast.143), channel_id=1, replica_groups=mesh['row'=8,'feat'=32] {'feat'}, dimensions={0} | all-to-all | bytes 1048576 | tf_op jit(solution)/shard_map/all_to_all | solution.py:79
  (75 shorter events, 23.0 us)
Async XLA Ops:
  0.0 25.3 %copy-start.1 = (bf16[32,1024]{1,0:T(8,128)(2,1)S(1)}, bf16[32,1024]{1,0:T(8,128)(2,1)}, u32[]{:S(2)}) copy-start(bf16[32,1024]{1,0:T(8,128)(2,1)} %param.15) | copy-start | bytes 196612
  0.0 67.2 %collective-permute-start.7 = (bf16[32,8192]{1,0:T(8,128)(2,1)}, bf16[32,8192]{1,0:T(8,128)(2,1)}, u32[]{:S(2)}, u32[]{:S(2)}) collective-permute-start(bf16[32,8192]{1,0:T(8,128)(2,1)} %param.10), channel_id=1, source_target_pairs={{0,96},{32,64},{64,32},{96,0},{128,224},{160,192},{192,160},{224,1... | collective-permute-start | bytes 1572872 | tf_op jit(solution)/shard_map/ppermute | solution.py:9
  3.6 67.8 %collective-permute-start.5 = (bf16[32,8192]{1,0:T(8,128)(2,1)}, bf16[32,8192]{1,0:T(8,128)(2,1)}, u32[]{:S(2)}, u32[]{:S(2)}) collective-permute-start(bf16[32,8192]{1,0:T(8,128)(2,1)} %param.10), channel_id=1, source_target_pairs={{0,32},{32,0},{64,96},{96,64},{128,160},{160,128},{192,224},{224,1... | collective-permute-start | bytes 1572872 | tf_op jit(solution)/shard_map/ppermute | solution.py:9
  4.9 18.5 %all-to-all-start = ((s32[8,1,32]{2,1,0:T(1,128)}), s32[8,1,32]{2,1,0:T(1,128)S(1)}, u32[]{:S(2)}, u32[]{:S(2)}) async-start(s32[8,1,32]{2,1,0:T(1,128)} %all_to_all.34), calls=%async_computation | async-start | bytes 8192 | tf_op jit(solution)/shard_map/all_to_all | solution.py:38
  10.1 15.2 %collective-permute-start = (bf16[1,32,1024]{2,1,0:T(8,128)(2,1)}, bf16[1,32,1024]{2,1,0:T(8,128)(2,1)S(1)}, u32[]{:S(2)}, u32[]{:S(2)}) collective-permute-start(bf16[1,32,1024]{2,1,0:T(8,128)(2,1)} %bitcast.145), channel_id=1, source_target_pairs={{0,16},{1,17},{2,18},{3,19},{4,20},{5,21},{6,22},{7,23},{8,24},{9,... | collective-permute-start | bytes 196616 | tf_op jit(solution)/shard_map/ppermute | solution.py:9
  25.1 26.1 %copy-start = (bf16[256,128,128]{2,1,0:T(8,128)(2,1)S(1)}, bf16[256,128,128]{2,1,0:T(8,128)(2,1)}, u32[]{:S(2)}) copy-start(bf16[256,128,128]{2,1,0:T(8,128)(2,1)} %param.11) | copy-start | bytes 25165828
  25.4 13.4 %collective-permute-start.1 = (bf16[2,32,1024]{2,1,0:T(8,128)(2,1)S(1)}, bf16[2,32,1024]{2,1,0:T(8,128)(2,1)S(1)}, u32[]{:S(2)}, u32[]{:S(2)}) collective-permute-start(bf16[2,32,1024]{2,1,0:T(8,128)(2,1)S(1)} %maximum_bitcast_fusion), channel_id=1, source_target_pairs={{0,8},{1,9},{2,10},{3,11},{4,12},{5,13},{6,14},{7,15},{8,0},{9,1},... | collective-permute-start | bytes 393224 | tf_op jit(solution)/shard_map/ppermute | solution.py:9
  32.6 10.1 %collective-permute-start.11 = (bf16[32,32,128]{2,1,0:T(8,128)(2,1)S(1)}, bf16[32,32,128]{2,1,0:T(8,128)(2,1)S(1)}, u32[]{:S(2)}, u32[]{:S(2)}) collective-permute-start(bf16[32,32,128]{2,1,0:T(8,128)(2,1)S(1)} %get-tuple-element.16), channel_id=1, source_target_pairs={{0,224},{32,192},{64,160},{96,128},{128,96},{160,64},{192,32},{224... | collective-permute-start | bytes 786440 | tf_op jit(solution)/shard_map/ppermute | solution.py:9
  38.4 10.2 %collective-permute-start.10 = (bf16[32,32,128]{2,1,0:T(8,128)(2,1)S(1)}, bf16[32,32,128]{2,1,0:T(8,128)(2,1)S(1)}, u32[]{:S(2)}, u32[]{:S(2)}) collective-permute-start(bf16[32,32,128]{2,1,0:T(8,128)(2,1)S(1)} %get-tuple-element.17), channel_id=1, source_target_pairs={{0,192},{32,224},{64,128},{96,160},{128,64},{160,96},{192,0},{224,... | collective-permute-start | bytes 786440 | tf_op jit(solution)/shard_map/ppermute | solution.py:9
  38.8 15.5 %collective-permute-start.9 = (bf16[32,32,128]{2,1,0:T(8,128)(2,1)S(1)}, bf16[32,32,128]{2,1,0:T(8,128)(2,1)S(1)}, u32[]{:S(2)}, u32[]{:S(2)}) collective-permute-start(bf16[32,32,128]{2,1,0:T(8,128)(2,1)S(1)} %get-tuple-element.18), channel_id=1, source_target_pairs={{0,160},{32,128},{64,224},{96,192},{128,32},{160,0},{192,96},{224,... | collective-permute-start | bytes 786440 | tf_op jit(solution)/shard_map/ppermute | solution.py:9
  42.7 17.0 %collective-permute-start.8 = (bf16[32,32,128]{2,1,0:T(8,128)(2,1)S(1)}, bf16[32,32,128]{2,1,0:T(8,128)(2,1)S(1)}, u32[]{:S(2)}, u32[]{:S(2)}) collective-permute-start(bf16[32,32,128]{2,1,0:T(8,128)(2,1)S(1)} %get-tuple-element.19), channel_id=1, source_target_pairs={{0,128},{32,160},{64,192},{96,224},{128,0},{160,32},{192,64},{224,... | collective-permute-start | bytes 786440 | tf_op jit(solution)/shard_map/ppermute | solution.py:9
  48.6 11.5 %collective-permute-start.6 = (bf16[32,32,128]{2,1,0:T(8,128)(2,1)S(1)}, bf16[32,32,128]{2,1,0:T(8,128)(2,1)S(1)}, u32[]{:S(2)}, u32[]{:S(2)}) collective-permute-start(bf16[32,32,128]{2,1,0:T(8,128)(2,1)S(1)} %get-tuple-element.20), channel_id=1, source_target_pairs={{0,64},{32,96},{64,0},{96,32},{128,192},{160,224},{192,128},{224,1... | collective-permute-start | bytes 786440 | tf_op jit(solution)/shard_map/ppermute | solution.py:9
  54.3 12.5 %collective-permute-start.2 = (bf16[4,32,1024]{2,1,0:T(8,128)(2,1)S(1)}, bf16[4,32,1024]{2,1,0:T(8,128)(2,1)S(1)}, u32[]{:S(2)}, u32[]{:S(2)}) collective-permute-start(bf16[4,32,1024]{2,1,0:T(8,128)(2,1)S(1)} %bitcast.141), channel_id=1, source_target_pairs={{0,4},{1,5},{2,6},{3,7},{4,0},{5,1},{6,2},{7,3},{8,12},{9,13},{10,... | collective-permute-start | bytes 786440 | tf_op jit(solution)/shard_map/ppermute | solution.py:9
  67.0 11.6 %collective-permute-start.3 = (bf16[8,32,1024]{2,1,0:T(8,128)(2,1)S(1)}, bf16[8,32,1024]{2,1,0:T(8,128)(2,1)}, u32[]{:S(2)}, u32[]{:S(2)}) collective-permute-start(bf16[8,32,1024]{2,1,0:T(8,128)(2,1)S(1)} %bitcast.138), channel_id=1, source_target_pairs={{0,2},{1,3},{2,0},{3,1},{4,6},{5,7},{6,4},{7,5},{8,10},{9,11},{10,... | collective-permute-start | bytes 1572872 | tf_op jit(solution)/shard_map/ppermute | solution.py:9
  79.8 9.5 %collective-permute-start.4 = (bf16[16,32,1024]{2,1,0:T(8,128)(2,1)S(1)}, bf16[16,32,1024]{2,1,0:T(8,128)(2,1)S(1)}, u32[]{:S(2)}, u32[]{:S(2)}) collective-permute-start(bf16[16,32,1024]{2,1,0:T(8,128)(2,1)S(1)} %bitcast.137), channel_id=1, source_target_pairs={{0,1},{1,0},{2,3},{3,2},{4,5},{5,4},{6,7},{7,6},{8,9},{9,8},{10,11... | collective-permute-start | bytes 3145736 | tf_op jit(solution)/shard_map/ppermute | solution.py:9
  83.4 22.4 %copy-start.2 = (f32[1024]{0:T(1024)S(1)}, f32[1024]{0:T(1024)}, u32[]{:S(2)}) copy-start(f32[1024]{0:T(1024)} %param.16) | copy-start | bytes 12292
  85.1 20.8 %all-to-all-start.1 = ((bf16[32,32,256]{2,0,1:T(8,128)(2,1)}), bf16[32,32,256]{2,0,1:T(8,128)(2,1)S(1)}, u32[]{:S(2)}, u32[]{:S(2)}) async-start(bf16[32,32,256]{2,0,1:T(8,128)(2,1)} %copy.65), calls=%async_computation.1 | async-start | bytes 1048576 | tf_op jit(solution)/shard_map/all_to_all | solution.py:76

commit v2 on v0

--- a/solution.py
+++ b/solution.py
@@ -9,20 +9,19 @@
     return lax.ppermute(value, axis, [(i, i ^ mask) for i in range(count)])
 
 
-def weight_bits():
-    bits = lax.axis_size("feat").bit_length() - 1
-    return [bits - 1] + list(range(bits - 2, 0, -1)) + [0]
-
-
-def gather_weight(held, bits):
+def gather_weight(weight):
+    feat_count = lax.axis_size("feat")
     me = lax.axis_index("feat")
-    for bit in bits:
+    bits = feat_count.bit_length() - 1
+    order = [bits - 1] + list(range(bits - 2, 0, -1)) + [0]
+    held = weight.reshape(1, -1, weight.shape[1])
+    for bit in order:
         theirs = swap_with(held, "feat", 1 << bit)
         mine_low = ((me >> bit) & 1) == 0
         low = jnp.where(mine_low, held, theirs)
         high = jnp.where(mine_low, theirs, held)
         held = jnp.stack([low, high], axis=1).reshape(-1, *held.shape[1:])
-    return held
+    return held.reshape(-1, weight.shape[1])
 
 
 def on_device(node_features, adjacency, tile_row, tile_col, tile_count, weight, out_bias):
@@ -35,10 +34,8 @@
     own_row = lax.axis_index("row")
     counts_here = tile_count[0]
 
-    bits = weight_bits()
-    w_mid = gather_weight(weight.reshape(1, *weight.shape), bits[:3])
+    w_full = gather_weight(weight)
     cols_out = lax.all_to_all(tile_col.reshape(cycle_len, slot_total), "row", 0, 0, tiled=True)
-    w_mid, cols_out = lax.optimization_barrier((w_mid, cols_out))
     blocks_t = node_features.reshape(feat_width, row_blocks, tile_size).transpose(1, 0, 2)
 
     tile_ids = jnp.arange(cycle_len * slot_total)
@@ -64,8 +61,6 @@
     running = add_source(running, jnp.take(blocks_t, own_cols, axis=0), own_row)
     for step_num in range(1, cycle_len):
         running = add_source(running, held[step_num - 1], jnp.bitwise_xor(own_row, step_num))
-    w_mid, _ = lax.optimization_barrier((gather_weight(w_mid, bits[3:4]), running))
-    w_full = gather_weight(w_mid, bits[4:]).reshape(-1, weight.shape[1])
     aggregated = running.reshape(feat_width, rows_here).astype(jnp.bfloat16)
     agg_t = lax.all_to_all(aggregated, "feat", 1, 0, tiled=True)
     pre_act = jnp.dot(w_full, agg_t, preferred_element_type=jnp.float32)

time: 132 us -> 132 us (level)
  matrix products: 18.2 us -> 11.4 us
  waiting for transfers between devices: 27.8 us -> 31.5 us
  starting transfers between devices: 44.4 us -> 47.8 us
    dot_general x8, matrix products: 13.6 us -> 6.74 us  [add_source(): jnp.einsum('sfj,sji->fsi', picked, tiles_part, preferred_element_type=jnp...]
    ppermute x12, waiting for transfers between devices: 13 us -> 16.7 us  [swap_with(): return lax.ppermute(value, axis, [(i, i ^ mask) for i in range(count)])]
    ppermute x12, starting transfers between devices: 31.4 us -> 34.4 us  [swap_with(): return lax.ppermute(value, axis, [(i, i ^ mask) for i in range(count)])]
  transfers between devices with their start and end apart: 14 -> 14, of which waited for: 5 -> 3; matrix products, arithmetic and copies ran while one was open for 24% -> 20% of each run, Pallas kernels for 0% -> 0%
where the time goes in v2:
time: 132 us; the launch traced here: 130 us
  starting transfers between devices  47.8 us (36%)
  waiting for transfers between devices  31.5 us (24%)
  blocking collectives  21.4 us (16%)
  matrix products  11.4 us (9%)
  local copies, waits for them, and re-layouts  9 us (7%)
  other arithmetic  8.31 us (6%)
    ppermute x12, starting transfers between devices, swap_with(): return lax.ppermute(value, axis, [(i, i ^ mask) for i in range(count)])  34.4 us
    all_to_all x1, blocking collectives, on_device(): activated = lax.all_to_all(act_t, 'feat', 0, 1, tiled=True)  21.4 us
    ppermute x12, waiting for transfers between devices, swap_with(): return lax.ppermute(value, axis, [(i, i ^ mask) for i in range(count)])  16.7 us
    all_to_all x1, waiting for transfers between devices, on_device(): agg_t = lax.all_to_all(aggregated, 'feat', 1, 0, tiled=True)  14.8 us
    all_to_all x1, starting transfers between devices, on_device(): lax.all_to_all(tile_col.reshape(cycle_len, slot_total), 'row', 0, 0, tile...  7.47 us
    dot_general x8, matrix products, add_source(): jnp.einsum('sfj,sji->fsi', picked, tiles_part, preferred_element_type=jnp...  6.74 us
    all_to_all x1, starting transfers between devices, on_device(): agg_t = lax.all_to_all(aggregated, 'feat', 1, 0, tiled=True)  5.93 us
    gather x3, other arithmetic, on_device(): live_all = tile_ids % slot_total < counts_here[tile_ids // slot_total]  5.01 us
  transfers between devices with their start and end apart: 14, of which 3 were waited for; matrix products, arithmetic and copies ran while one was open for 20% of the time, Pallas kernels for 0%

profile of v2, /device:TPU:1, one launch (start us, length us, event | category | flops | bytes accessed | tf_op | source)
XLA Modules:
  0.0 129.9 jit_solution(4840599006395470233)
XLA Ops:
  0.0 1.4 %all_to_all.34 = s32[8,1,32]{2,1,0:T(1,128)} reshape(s32[256]{0:T(256)} %param.10) | data formatting | bytes 2048 | tf_op jit(solution)/shard_map/all_to_all | solution.py:38
  1.4 7.5 %all-to-all-start = ((s32[8,1,32]{2,1,0:T(1,128)}), s32[8,1,32]{2,1,0:T(1,128)S(1)}, u32[]{:S(2)}, u32[]{:S(2)}) async-start(s32[8,1,32]{2,1,0:T(1,128)} %all_to_all.34), calls=%async_computation | async-start | bytes 8192 | tf_op jit(solution)/shard_map/all_to_all | solution.py:38
  10.2 1.6 %fusion.64 = (s32[1,1]{1,0:T(1,128)}, s32[1,1]{1,0:T(1,128)}, s32[1,1]{1,0:T(1,128)}, s32[1,1]{1,0:T(1,128)}, s32[1,1]{1,0:T(1,128)}, /*index=5*/s32[1,1]{1,0:T(1,128)}, s32[1,1]{1,0:T(1,128)}, s32[1,1]{1,0:T(1,128)}) fusion(s32[1,8]{1,0:T(1,128)} %param.11), kind=kLoop, calls=%fused_computation.128 | loop fusion | bytes 64 | tf_op jit(solution)/shard_map/gather | solution.py:42
  11.8 4.3 %compare_select_fusion.2 = s32[256,1]{0,1:T(1,128)S(1)} fusion(s32[]{:T(128)} %bitcast.18, s32[]{:T(128)} %bitcast.19, s32[]{:T(128)} %bitcast.20, s32[]{:T(128)} %bitcast.21, s32[]{:T(128)} %bitcast.22, s32[]{:T(128)} %bitcast.24, s32[]{:T(128)} %bitcast.23), kind=kLoop, calls=%fused_computation.106 | loop fusion | flops 5888 | bytes 1052 | tf_op jit(solution)/shard_map/gather | solution.py:42
  18.4 1.7 %convolution_bitcast_fusion.7 = bf16[32,32,128]{2,0,1:T(8,128)(2,1)S(1)} fusion(bf16[256,128,128]{2,1,0:T(8,128)(2,1)} %param.8, s32[]{:T(128)S(6)} %select_n.227, bf16[32,32,128]{2,1,0:T(8,128)(2,1)S(1)} %gather_fusion, pred[32]{0:T(512)(128)(4,1)S(1)} %get-tuple-element.5), kind=kOutput, calls=%fused_computation.24 | convolution fusion | flops 33685504 | bytes 1572900 | tf_op jit(solution)/shard_map/sfj,sji->fsi/dot_general | solution.py:50
  20.1 1.4 %fusion.19 = f32[64,32,128]{2,0,1:T(8,128)} fusion(bf16[32,32,128]{2,0,1:T(8,128)(2,1)S(1)} %convolution_bitcast_fusion.7, pred[8,32,64]{2,1,0:T(32,128)(4,1)S(1)} %fusion.24, s32[]{:T(128)S(6)} %select_n.226), kind=kOutput, calls=%fused_computation.45 | convolution fusion | flops 16777216 | bytes 1314820 | tf_op jit(solution)/shard_map/fsi,sr->fri/dot_general | solution.py:51
  22.3 1.0 gather_fusion.2
  23.7 7.0 %collective-permute-start.1 = (bf16[2,32,1024]{2,1,0:T(8,128)(2,1)S(1)}, bf16[2,32,1024]{2,1,0:T(8,128)(2,1)S(1)}, u32[]{:S(2)}, u32[]{:S(2)}) collective-permute-start(bf16[2,32,1024]{2,1,0:T(8,128)(2,1)S(1)} %maximum_bitcast_fusion), channel_id=1, source_target_pairs={{0,8},{1,9},{2,10},{3,11},{4,12},{5,13},{6,14},{7,15},{8,0},{9,1},... | collective-permute-start | bytes 393224 | tf_op jit(solution)/shard_map/ppermute | solution.py:9
  31.0 1.6 %collective-permute-start.5 = (bf16[32,32,128]{2,1,0:T(8,128)(2,1)S(1)}, bf16[32,32,128]{2,1,0:T(8,128)(2,1)S(1)}, u32[]{:S(2)}, u32[]{:S(2)}) collective-permute-start(bf16[32,32,128]{2,1,0:T(8,128)(2,1)S(1)} %get-tuple-element.15), channel_id=1, source_target_pairs={{0,32},{32,0},{64,96},{96,64},{128,160},{160,128},{192,224},{224,1... | collective-permute-start | bytes 786440 | tf_op jit(solution)/shard_map/ppermute | solution.py:9
  32.5 2.4 %collective-permute-start.6 = (bf16[32,32,128]{2,1,0:T(8,128)(2,1)S(1)}, bf16[32,32,128]{2,1,0:T(8,128)(2,1)S(1)}, u32[]{:S(2)}, u32[]{:S(2)}) collective-permute-start(bf16[32,32,128]{2,1,0:T(8,128)(2,1)S(1)} %get-tuple-element.14), channel_id=1, source_target_pairs={{0,64},{32,96},{64,0},{96,32},{128,192},{160,224},{192,128},{224,1... | collective-permute-start | bytes 786440 | tf_op jit(solution)/shard_map/ppermute | solution.py:9
  35.0 3.5 %collective-permute-start.8 = (bf16[32,32,128]{2,1,0:T(8,128)(2,1)S(1)}, bf16[32,32,128]{2,1,0:T(8,128)(2,1)S(1)}, u32[]{:S(2)}, u32[]{:S(2)}) collective-permute-start(bf16[32,32,128]{2,1,0:T(8,128)(2,1)S(1)} %get-tuple-element.12), channel_id=1, source_target_pairs={{0,128},{32,160},{64,192},{96,224},{128,0},{160,32},{192,64},{224,... | collective-permute-start | bytes 786440 | tf_op jit(solution)/shard_map/ppermute | solution.py:9
  38.6 6.1 %collective-permute-start.10 = (bf16[32,32,128]{2,1,0:T(8,128)(2,1)S(1)}, bf16[32,32,128]{2,1,0:T(8,128)(2,1)S(1)}, u32[]{:S(2)}, u32[]{:S(2)}) collective-permute-start(bf16[32,32,128]{2,1,0:T(8,128)(2,1)S(1)} %get-tuple-element.10), channel_id=1, source_target_pairs={{0,192},{32,224},{64,128},{96,160},{128,64},{160,96},{192,0},{224,... | collective-permute-start | bytes 786440 | tf_op jit(solution)/shard_map/ppermute | solution.py:9
  44.7 1.6 %convolution_bitcast_fusion.6 = bf16[32,32,128]{2,0,1:T(8,128)(2,1)S(1)} fusion(bf16[32,32,128]{2,1,0:T(8,128)(2,1)S(1)} %collective-permute-done.5, bf16[256,128,128]{2,1,0:T(8,128)(2,1)} %param.8, s32[]{:T(128)S(6)} %select_n.231), kind=kOutput, calls=%fused_computation.23 | convolution fusion | flops 33554432 | bytes 1572868 | tf_op jit(solution)/shard_map/sfj,sji->fsi/dot_general | solution.py:50
  46.7 3.2 %collective-permute-start.11 = (bf16[32,32,128]{2,1,0:T(8,128)(2,1)S(1)}, bf16[32,32,128]{2,1,0:T(8,128)(2,1)S(1)}, u32[]{:S(2)}, u32[]{:S(2)}) collective-permute-start(bf16[32,32,128]{2,1,0:T(8,128)(2,1)S(1)} %get-tuple-element.9), channel_id=1, source_target_pairs={{0,224},{32,192},{64,160},{96,128},{128,96},{160,64},{192,32},{224... | collective-permute-start | bytes 786440 | tf_op jit(solution)/shard_map/ppermute | solution.py:9
  49.8 1.6 %convolution_bitcast_fusion.5 = bf16[32,32,128]{2,0,1:T(8,128)(2,1)S(1)} fusion(bf16[32,32,128]{2,1,0:T(8,128)(2,1)S(1)} %collective-permute-done.6, bf16[256,128,128]{2,1,0:T(8,128)(2,1)} %param.8, s32[]{:T(128)S(6)} %select_n.241), kind=kOutput, calls=%fused_computation.22 | convolution fusion | flops 33554432 | bytes 1572868 | tf_op jit(solution)/shard_map/sfj,sji->fsi/dot_general | solution.py:50
  53.8 7.0 %collective-permute-done.2 = bf16[4,32,1024]{2,1,0:T(8,128)(2,1)S(1)} collective-permute-done((bf16[4,32,1024]{2,1,0:T(8,128)(2,1)S(1)}, bf16[4,32,1024]{2,1,0:T(8,128)(2,1)S(1)}, u32[]{:S(2)}, u32[]{:S(2)}) %collective-permute-start.2) | collective-permute-done | bytes 262176 | tf_op jit(solution)/shard_map/ppermute | solution.py:9
  62.5 9.7 %collective-permute-done.3 = bf16[8,32,1024]{2,1,0:T(8,128)(2,1)S(1)} collective-permute-done((bf16[8,32,1024]{2,1,0:T(8,128)(2,1)S(1)}, bf16[8,32,1024]{2,1,0:T(8,128)(2,1)S(1)}, u32[]{:S(2)}, u32[]{:S(2)}) %collective-permute-start.3) | collective-permute-done | bytes 524320 | tf_op jit(solution)/shard_map/ppermute | solution.py:9
  72.4 9.6 %collective-permute-start.4 = (bf16[16,32,1024]{2,1,0:T(8,128)(2,1)S(1)}, bf16[16,32,1024]{2,1,0:T(8,128)(2,1)}, u32[]{:S(2)}, u32[]{:S(2)}) collective-permute-start(bf16[16,32,1024]{2,1,0:T(8,128)(2,1)S(1)} %bitcast.129), channel_id=1, source_target_pairs={{0,1},{1,0},{2,3},{3,2},{4,5},{5,4},{6,7},{7,6},{8,9},{9,8},{10,11... | collective-permute-start | bytes 3145736 | tf_op jit(solution)/shard_map/ppermute | solution.py:9
  83.4 1.1 copy.58
  84.5 5.9 %all-to-all-start.1 = ((bf16[32,32,256]{2,0,1:T(8,128)(2,1)}), bf16[32,32,256]{2,0,1:T(8,128)(2,1)S(1)}, u32[]{:S(2)}, u32[]{:S(2)}) async-start(bf16[32,32,256]{2,0,1:T(8,128)(2,1)} %copy.58), calls=%async_computation.1 | async-start | bytes 1048576 | tf_op jit(solution)/shard_map/all_to_all | solution.py:65
  90.4 1.4 %select_bitcast_fusion.1 = (bf16[16,1,32,1024]{3,2,0,1:T(8,128)(2,1)S(1)}, bf16[16,1,32,1024]{3,2,0,1:T(8,128)(2,1)S(1)}) fusion(bf16[16,32,1024]{2,1,0:T(8,128)(2,1)} %collective-permute-done.4, pred[]{:T(512)S(6)} %eq.33, bf16[8,2,32,1024]{3,2,1,0:T(8,128)(2,1)S(1)} %copy.47), kind=kLoop, calls=%fused_computation.35 | loop fusion | flops 1048576 | bytes 4194305 | tf_op jit(solution)/shard_map/stack | solution.py:23
  92.2 14.8 %all-to-all-done.1 = bf16[32,32,256]{2,0,1:T(8,128)(2,1)S(1)} async-done(((bf16[32,32,256]{2,0,1:T(8,128)(2,1)}), bf16[32,32,256]{2,0,1:T(8,128)(2,1)S(1)}, u32[]{:S(2)}, u32[]{:S(2)}) %all-to-all-start.1) | async-done | bytes 524320 | tf_op jit(solution)/shard_map/all_to_all | solution.py:65
  107.7 21.4 %all_to_all.47 = bf16[32,32,256]{2,1,0:T(8,128)(2,1)S(1)} all-to-all(bf16[32,32,256]{2,1,0:T(8,128)(2,1)S(1)} %bitcast.135), channel_id=1, replica_groups=mesh['row'=8,'feat'=32] {'feat'}, dimensions={0} | all-to-all | bytes 1048576 | tf_op jit(solution)/shard_map/all_to_all | solution.py:68
  129.1 0.8 copy.61
  (77 shorter events, 12.0 us)
Async XLA Ops:
  0.0 10.1 %copy-start = (bf16[32,8192]{1,0:T(8,128)(2,1)S(1)}, bf16[32,8192]{1,0:T(8,128)(2,1)}, u32[]{:S(2)}) copy-start(bf16[32,8192]{1,0:T(8,128)(2,1)} %param.7) | copy-start | bytes 1572868
  0.0 23.6 %copy-start.2 = (bf16[32,1024]{1,0:T(8,128)(2,1)S(1)}, bf16[32,1024]{1,0:T(8,128)(2,1)}, u32[]{:S(2)}) copy-start(bf16[32,1024]{1,0:T(8,128)(2,1)} %param.12) | copy-start | bytes 196612
  1.4 20.1 %all-to-all-start = ((s32[8,1,32]{2,1,0:T(1,128)}), s32[8,1,32]{2,1,0:T(1,128)S(1)}, u32[]{:S(2)}, u32[]{:S(2)}) async-start(s32[8,1,32]{2,1,0:T(1,128)} %all_to_all.34), calls=%async_computation | async-start | bytes 8192 | tf_op jit(solution)/shard_map/all_to_all | solution.py:38
  8.9 14.7 %collective-permute-start = (bf16[1,32,1024]{2,1,0:T(8,128)(2,1)}, bf16[1,32,1024]{2,1,0:T(8,128)(2,1)S(1)}, u32[]{:S(2)}, u32[]{:S(2)}) collective-permute-start(bf16[1,32,1024]{2,1,0:T(8,128)(2,1)} %bitcast.137), channel_id=1, source_target_pairs={{0,16},{1,17},{2,18},{3,19},{4,20},{5,21},{6,22},{7,23},{8,24},{9,... | collective-permute-start | bytes 196616 | tf_op jit(solution)/shard_map/ppermute | solution.py:9
  23.2 23.0 %copy-start.1 = (f32[64,32,128]{2,0,1:T(8,128)S(1)}, f32[64,32,128]{2,0,1:T(8,128)}, u32[]{:S(2)}) copy-start(f32[64,32,128]{2,0,1:T(8,128)} %fusion.19) | copy-start | bytes 3145732
  23.3 29.0 %slice-start = ((s8[8388608]{0:T(1024)(128)(4,1)}), s8[4194304]{0:T(1024)(128)(4,1)S(1)}, s32[]{:S(2)}) async-start(s8[8388608]{0:T(1024)(128)(4,1)} %bitcast.127), calls=%async_computation.3 | async-start | bytes 8388608
  23.7 14.9 %collective-permute-start.1 = (bf16[2,32,1024]{2,1,0:T(8,128)(2,1)S(1)}, bf16[2,32,1024]{2,1,0:T(8,128)(2,1)S(1)}, u32[]{:S(2)}, u32[]{:S(2)}) collective-permute-start(bf16[2,32,1024]{2,1,0:T(8,128)(2,1)S(1)} %maximum_bitcast_fusion), channel_id=1, source_target_pairs={{0,8},{1,9},{2,10},{3,11},{4,12},{5,13},{6,14},{7,15},{8,0},{9,1},... | collective-permute-start | bytes 393224 | tf_op jit(solution)/shard_map/ppermute | solution.py:9
  31.0 7.6 %collective-permute-start.5 = (bf16[32,32,128]{2,1,0:T(8,128)(2,1)S(1)}, bf16[32,32,128]{2,1,0:T(8,128)(2,1)S(1)}, u32[]{:S(2)}, u32[]{:S(2)}) collective-permute-start(bf16[32,32,128]{2,1,0:T(8,128)(2,1)S(1)} %get-tuple-element.15), channel_id=1, source_target_pairs={{0,32},{32,0},{64,96},{96,64},{128,160},{160,128},{192,224},{224,1... | collective-permute-start | bytes 786440 | tf_op jit(solution)/shard_map/ppermute | solution.py:9
  32.5 14.1 %collective-permute-start.6 = (bf16[32,32,128]{2,1,0:T(8,128)(2,1)S(1)}, bf16[32,32,128]{2,1,0:T(8,128)(2,1)S(1)}, u32[]{:S(2)}, u32[]{:S(2)}) collective-permute-start(bf16[32,32,128]{2,1,0:T(8,128)(2,1)S(1)} %get-tuple-element.14), channel_id=1, source_target_pairs={{0,64},{32,96},{64,0},{96,32},{128,192},{160,224},{192,128},{224,1... | collective-permute-start | bytes 786440 | tf_op jit(solution)/shard_map/ppermute | solution.py:9
  34.9 16.9 %collective-permute-start.7 = (bf16[32,32,128]{2,1,0:T(8,128)(2,1)S(1)}, bf16[32,32,128]{2,1,0:T(8,128)(2,1)S(1)}, u32[]{:S(2)}, u32[]{:S(2)}) collective-permute-start(bf16[32,32,128]{2,1,0:T(8,128)(2,1)S(1)} %get-tuple-element.13), channel_id=1, source_target_pairs={{0,96},{32,64},{64,32},{96,0},{128,224},{160,192},{192,160},{224,1... | collective-permute-start | bytes 786440 | tf_op jit(solution)/shard_map/ppermute | solution.py:9
  35.0 18.0 %collective-permute-start.8 = (bf16[32,32,128]{2,1,0:T(8,128)(2,1)S(1)}, bf16[32,32,128]{2,1,0:T(8,128)(2,1)S(1)}, u32[]{:S(2)}, u32[]{:S(2)}) collective-permute-start(bf16[32,32,128]{2,1,0:T(8,128)(2,1)S(1)} %get-tuple-element.12), channel_id=1, source_target_pairs={{0,128},{32,160},{64,192},{96,224},{128,0},{160,32},{192,64},{224,... | collective-permute-start | bytes 786440 | tf_op jit(solution)/shard_map/ppermute | solution.py:9
  38.5 22.8 %collective-permute-start.9 = (bf16[32,32,128]{2,1,0:T(8,128)(2,1)S(1)}, bf16[32,32,128]{2,1,0:T(8,128)(2,1)S(1)}, u32[]{:S(2)}, u32[]{:S(2)}) collective-permute-start(bf16[32,32,128]{2,1,0:T(8,128)(2,1)S(1)} %get-tuple-element.11), channel_id=1, source_target_pairs={{0,160},{32,128},{64,224},{96,192},{128,32},{160,0},{192,96},{224,... | collective-permute-start | bytes 786440 | tf_op jit(solution)/shard_map/ppermute | solution.py:9
  38.5 13.8 %slice-start.1 = ((s8[8388608]{0:T(1024)(128)(4,1)}), s8[4194304]{0:T(1024)(128)(4,1)S(1)}, s32[]{:S(2)}) async-start(s8[8388608]{0:T(1024)(128)(4,1)} %bitcast.127), calls=%async_computation.4 | async-start | bytes 8388608
  38.6 23.1 %collective-permute-start.10 = (bf16[32,32,128]{2,1,0:T(8,128)(2,1)S(1)}, bf16[32,32,128]{2,1,0:T(8,128)(2,1)S(1)}, u32[]{:S(2)}, u32[]{:S(2)}) collective-permute-start(bf16[32,32,128]{2,1,0:T(8,128)(2,1)S(1)} %get-tuple-element.10), channel_id=1, source_target_pairs={{0,192},{32,224},{64,128},{96,160},{128,64},{160,96},{192,0},{224,... | collective-permute-start | bytes 786440 | tf_op jit(solution)/shard_map/ppermute | solution.py:9
  46.7 35.8 %collective-permute-start.11 = (bf16[32,32,128]{2,1,0:T(8,128)(2,1)S(1)}, bf16[32,32,128]{2,1,0:T(8,128)(2,1)S(1)}, u32[]{:S(2)}, u32[]{:S(2)}) collective-permute-start(bf16[32,32,128]{2,1,0:T(8,128)(2,1)S(1)} %get-tuple-element.9), channel_id=1, source_target_pairs={{0,224},{32,192},{64,160},{96,128},{128,96},{160,64},{192,32},{224... | collective-permute-start | bytes 786440 | tf_op jit(solution)/shard_map/ppermute | solution.py:9
  51.8 9.0 %collective-permute-start.2 = (bf16[4,32,1024]{2,1,0:T(8,128)(2,1)S(1)}, bf16[4,32,1024]{2,1,0:T(8,128)(2,1)S(1)}, u32[]{:S(2)}, u32[]{:S(2)}) collective-permute-start(bf16[4,32,1024]{2,1,0:T(8,128)(2,1)S(1)} %bitcast.133), channel_id=1, source_target_pairs={{0,4},{1,5},{2,6},{3,7},{4,0},{5,1},{6,2},{7,3},{8,12},{9,13},{10,... | collective-permute-start | bytes 786440 | tf_op jit(solution)/shard_map/ppermute | solution.py:9
  61.0 11.1 %collective-permute-start.3 = (bf16[8,32,1024]{2,1,0:T(8,128)(2,1)S(1)}, bf16[8,32,1024]{2,1,0:T(8,128)(2,1)S(1)}, u32[]{:S(2)}, u32[]{:S(2)}) collective-permute-start(bf16[8,32,1024]{2,1,0:T(8,128)(2,1)S(1)} %bitcast.130), channel_id=1, source_target_pairs={{0,2},{1,3},{2,0},{3,1},{4,6},{5,7},{6,4},{7,5},{8,10},{9,11},{10,... | collective-permute-start | bytes 1572872 | tf_op jit(solution)/shard_map/ppermute | solution.py:9
  72.4 18.0 %collective-permute-start.4 = (bf16[16,32,1024]{2,1,0:T(8,128)(2,1)S(1)}, bf16[16,32,1024]{2,1,0:T(8,128)(2,1)}, u32[]{:S(2)}, u32[]{:S(2)}) collective-permute-start(bf16[16,32,1024]{2,1,0:T(8,128)(2,1)S(1)} %bitcast.129), channel_id=1, source_target_pairs={{0,1},{1,0},{2,3},{3,2},{4,5},{5,4},{6,7},{7,6},{8,9},{9,8},{10,11... | collective-permute-start | bytes 3145736 | tf_op jit(solution)/shard_map/ppermute | solution.py:9
  82.8 24.2 %copy-start.3 = (f32[1024]{0:T(1024)S(1)}, f32[1024]{0:T(1024)}, u32[]{:S(2)}) copy-start(f32[1024]{0:T(1024)} %param.13) | copy-start | bytes 12292
  84.5 22.5 %all-to-all-start.1 = ((bf16[32,32,256]{2,0,1:T(8,128)(2,1)}), bf16[32,32,256]{2,0,1:T(8,128)(2,1)S(1)}, u32[]{:S(2)}, u32[]{:S(2)}) async-start(bf16[32,32,256]{2,0,1:T(8,128)(2,1)} %copy.58), calls=%async_computation.1 | async-start | bytes 1048576 | tf_op jit(solution)/shard_map/all_to_all | solution.py:65

commit v3 on v0

--- a/solution.py
+++ b/solution.py
@@ -36,9 +36,10 @@
     counts_here = tile_count[0]
 
     bits = weight_bits()
-    w_mid = gather_weight(weight.reshape(1, *weight.shape), bits[:3])
+    w_mid = gather_weight(weight.reshape(1, *weight.shape), bits[:2])
     cols_out = lax.all_to_all(tile_col.reshape(cycle_len, slot_total), "row", 0, 0, tiled=True)
     w_mid, cols_out = lax.optimization_barrier((w_mid, cols_out))
+    w_full = gather_weight(w_mid, bits[2:]).reshape(-1, weight.shape[1])
     blocks_t = node_features.reshape(feat_width, row_blocks, tile_size).transpose(1, 0, 2)
 
     tile_ids = jnp.arange(cycle_len * slot_total)
@@ -64,8 +65,6 @@
     running = add_source(running, jnp.take(blocks_t, own_cols, axis=0), own_row)
     for step_num in range(1, cycle_len):
         running = add_source(running, held[step_num - 1], jnp.bitwise_xor(own_row, step_num))
-    w_mid, _ = lax.optimization_barrier((gather_weight(w_mid, bits[3:4]), running))
-    w_full = gather_weight(w_mid, bits[4:]).reshape(-1, weight.shape[1])
     aggregated = running.reshape(feat_width, rows_here).astype(jnp.bfloat16)
     agg_t = lax.all_to_all(aggregated, "feat", 1, 0, tiled=True)
     pre_act = jnp.dot(w_full, agg_t, preferred_element_type=jnp.float32)

time: 132 us -> 129 us (0.977)
  starting transfers between devices: 44.4 us -> 51.8 us
  matrix products: 18.2 us -> 11.4 us
  waiting for transfers between devices: 27.8 us -> 24.3 us
    ppermute x12, starting transfers between devices: 31.4 us -> 41.8 us  [swap_with(): return lax.ppermute(value, axis, [(i, i ^ mask) for i in range(count)])]
    dot_general x8, matrix products: 13.6 us -> 6.74 us  [add_source(): jnp.einsum('sfj,sji->fsi', picked, tiles_part, preferred_element_type=jnp...]
    ppermute x12, waiting for transfers between devices: 13 us -> 9.45 us  [swap_with(): return lax.ppermute(value, axis, [(i, i ^ mask) for i in range(count)])]
    all_to_all x1, starting transfers between devices: 6.64 us -> 3.68 us  [on_device(): agg_t = lax.all_to_all(aggregated, 'feat', 1, 0, tiled=True)]
  transfers between devices with their start and end apart: 14 -> 14, of which waited for: 5 -> 5; matrix products, arithmetic and copies ran while one was open for 24% -> 19% of each run, Pallas kernels for 0% -> 0%
where the time goes in v3:
time: 129 us; the launch traced here: 127 us
  starting transfers between devices  51.8 us (40%)
  waiting for transfers between devices  24.3 us (19%)
  blocking collectives  21.4 us (17%)
  matrix products  11.4 us (9%)
  other arithmetic  9.14 us (7%)
  local copies, waits for them, and re-layouts  8.94 us (7%)
    ppermute x12, starting transfers between devices, swap_with(): return lax.ppermute(value, axis, [(i, i ^ mask) for i in range(count)])  41.8 us
    all_to_all x1, blocking collectives, on_device(): activated = lax.all_to_all(act_t, 'feat', 0, 1, tiled=True)  21.4 us
    all_to_all x1, waiting for transfers between devices, on_device(): agg_t = lax.all_to_all(aggregated, 'feat', 1, 0, tiled=True)  14.8 us
    ppermute x12, waiting for transfers between devices, swap_with(): return lax.ppermute(value, axis, [(i, i ^ mask) for i in range(count)])  9.45 us
    dot_general x8, matrix products, add_source(): jnp.einsum('sfj,sji->fsi', picked, tiles_part, preferred_element_type=jnp...  6.74 us
    all_to_all x1, starting transfers between devices, on_device(): lax.all_to_all(tile_col.reshape(cycle_len, slot_total), 'row', 0, 0, tile...  6.36 us
    gather x3, other arithmetic, on_device(): live_all = tile_ids % slot_total < counts_here[tile_ids // slot_total]  5.03 us
    dot_general x8, matrix products, add_source(): return running + jnp.einsum('fsi,sr->fri', product, onehot)  3.97 us
  transfers between devices with their start and end apart: 14, of which 5 were waited for; matrix products, arithmetic and copies ran while one was open for 19% of the time, Pallas kernels for 0%

profile of v3, /device:TPU:1, one launch (start us, length us, event | category | flops | bytes accessed | tf_op | source)
XLA Modules:
  0.0 127.4 jit_solution(1129701943900413596)
XLA Ops:
  0.0 2.0 %collective-permute-start = (bf16[1,32,1024]{2,1,0:T(8,128)(2,1)}, bf16[1,32,1024]{2,1,0:T(8,128)(2,1)S(1)}, u32[]{:S(2)}, u32[]{:S(2)}) collective-permute-start(bf16[1,32,1024]{2,1,0:T(8,128)(2,1)} %bitcast.136), channel_id=1, source_target_pairs={{0,16},{1,17},{2,18},{3,19},{4,20},{5,21},{6,22},{7,23},{8,24},{9,... | collective-permute-start | bytes 196616 | tf_op jit(solution)/shard_map/ppermute | solution.py:9
  3.4 6.4 %all-to-all-start = ((s32[8,1,32]{2,1,0:T(1,128)}), s32[8,1,32]{2,1,0:T(1,128)S(1)}, u32[]{:S(2)}, u32[]{:S(2)}) async-start(s32[8,1,32]{2,1,0:T(1,128)} %all_to_all.34), calls=%async_computation | async-start | bytes 8192 | tf_op jit(solution)/shard_map/all_to_all | solution.py:40
  10.7 1.6 %fusion.64 = (s32[1,1]{1,0:T(1,128)}, s32[1,1]{1,0:T(1,128)}, s32[1,1]{1,0:T(1,128)}, s32[1,1]{1,0:T(1,128)}, s32[1,1]{1,0:T(1,128)}, /*index=5*/s32[1,1]{1,0:T(1,128)}, s32[1,1]{1,0:T(1,128)}, s32[1,1]{1,0:T(1,128)}) fusion(s32[1,8]{1,0:T(1,128)} %param.11), kind=kLoop, calls=%fused_computation.128 | loop fusion | bytes 64 | tf_op jit(solution)/shard_map/gather | solution.py:46
  12.3 4.3 %compare_select_fusion.2 = s32[256,1]{0,1:T(1,128)S(1)} fusion(s32[]{:T(128)} %bitcast.19, s32[]{:T(128)} %bitcast.20, s32[]{:T(128)} %bitcast.21, s32[]{:T(128)} %bitcast.22, s32[]{:T(128)} %bitcast.23, s32[]{:T(128)} %bitcast.25, s32[]{:T(128)} %bitcast.24), kind=kLoop, calls=%fused_computation.106 | loop fusion | flops 5888 | bytes 1052 | tf_op jit(solution)/shard_map/gather | solution.py:46
  18.9 1.7 %convolution_bitcast_fusion.7 = bf16[32,32,128]{2,0,1:T(8,128)(2,1)S(1)} fusion(bf16[256,128,128]{2,1,0:T(8,128)(2,1)} %param.8, s32[]{:T(128)S(6)} %select_n.227, bf16[32,32,128]{2,1,0:T(8,128)(2,1)S(1)} %gather_fusion, pred[32]{0:T(512)(128)(4,1)S(1)} %get-tuple-element.9), kind=kOutput, calls=%fused_computation.24 | convolution fusion | flops 33685504 | bytes 1572900 | tf_op jit(solution)/shard_map/sfj,sji->fsi/dot_general | solution.py:54
  20.6 1.4 %fusion.19 = f32[64,32,128]{2,0,1:T(8,128)} fusion(bf16[32,32,128]{2,0,1:T(8,128)(2,1)S(1)} %convolution_bitcast_fusion.7, pred[8,32,64]{2,1,0:T(32,128)(4,1)S(1)} %fusion.24, s32[]{:T(128)S(6)} %select_n.226), kind=kOutput, calls=%fused_computation.45 | convolution fusion | flops 16777216 | bytes 1314820 | tf_op jit(solution)/shard_map/fsi,sr->fri/dot_general | solution.py:55
  22.8 7.0 %collective-permute-start.1 = (bf16[2,32,1024]{2,1,0:T(8,128)(2,1)S(1)}, bf16[2,32,1024]{2,1,0:T(8,128)(2,1)S(1)}, u32[]{:S(2)}, u32[]{:S(2)}) collective-permute-start(bf16[2,32,1024]{2,1,0:T(8,128)(2,1)S(1)} %maximum_bitcast_fusion), channel_id=1, source_target_pairs={{0,8},{1,9},{2,10},{3,11},{4,12},{5,13},{6,14},{7,15},{8,0},{9,1},... | collective-permute-start | bytes 393224 | tf_op jit(solution)/shard_map/ppermute | solution.py:9
  29.8 2.4 %collective-permute-done.1 = bf16[2,32,1024]{2,1,0:T(8,128)(2,1)S(1)} collective-permute-done((bf16[2,32,1024]{2,1,0:T(8,128)(2,1)S(1)}, bf16[2,32,1024]{2,1,0:T(8,128)(2,1)S(1)}, u32[]{:S(2)}, u32[]{:S(2)}) %collective-permute-start.1) | collective-permute-done | bytes 131104 | tf_op jit(solution)/shard_map/ppermute | solution.py:9
  34.2 5.2 %collective-permute-start.2 = (bf16[4,32,1024]{2,1,0:T(8,128)(2,1)S(1)}, bf16[4,32,1024]{2,1,0:T(8,128)(2,1)S(1)}, u32[]{:S(2)}, u32[]{:S(2)}) collective-permute-start(bf16[4,32,1024]{2,1,0:T(8,128)(2,1)S(1)} %bitcast.131), channel_id=1, source_target_pairs={{0,4},{1,5},{2,6},{3,7},{4,0},{5,1},{6,2},{7,3},{8,12},{9,13},{10,... | collective-permute-start | bytes 786440 | tf_op jit(solution)/shard_map/ppermute | solution.py:9
  40.0 1.5 %collective-permute-start.5 = (bf16[32,32,128]{2,1,0:T(8,128)(2,1)S(1)}, bf16[32,32,128]{2,1,0:T(8,128)(2,1)S(1)}, u32[]{:S(2)}, u32[]{:S(2)}) collective-permute-start(bf16[32,32,128]{2,1,0:T(8,128)(2,1)S(1)} %get-tuple-element.19), channel_id=1, source_target_pairs={{0,32},{32,0},{64,96},{96,64},{128,160},{160,128},{192,224},{224,1... | collective-permute-start | bytes 786440 | tf_op jit(solution)/shard_map/ppermute | solution.py:9
  41.6 2.4 %collective-permute-start.6 = (bf16[32,32,128]{2,1,0:T(8,128)(2,1)S(1)}, bf16[32,32,128]{2,1,0:T(8,128)(2,1)S(1)}, u32[]{:S(2)}, u32[]{:S(2)}) collective-permute-start(bf16[32,32,128]{2,1,0:T(8,128)(2,1)S(1)} %get-tuple-element.18), channel_id=1, source_target_pairs={{0,64},{32,96},{64,0},{96,32},{128,192},{160,224},{192,128},{224,1... | collective-permute-start | bytes 786440 | tf_op jit(solution)/shard_map/ppermute | solution.py:9
  44.1 2.9 %collective-permute-start.8 = (bf16[32,32,128]{2,1,0:T(8,128)(2,1)S(1)}, bf16[32,32,128]{2,1,0:T(8,128)(2,1)S(1)}, u32[]{:S(2)}, u32[]{:S(2)}) collective-permute-start(bf16[32,32,128]{2,1,0:T(8,128)(2,1)S(1)} %get-tuple-element.16), channel_id=1, source_target_pairs={{0,128},{32,160},{64,192},{96,224},{128,0},{160,32},{192,64},{224,... | collective-permute-start | bytes 786440 | tf_op jit(solution)/shard_map/ppermute | solution.py:9
  47.0 1.7 %collective-permute-done.2 = bf16[4,32,1024]{2,1,0:T(8,128)(2,1)S(1)} collective-permute-done((bf16[4,32,1024]{2,1,0:T(8,128)(2,1)S(1)}, bf16[4,32,1024]{2,1,0:T(8,128)(2,1)S(1)}, u32[]{:S(2)}, u32[]{:S(2)}) %collective-permute-start.2) | collective-permute-done | bytes 262176 | tf_op jit(solution)/shard_map/ppermute | solution.py:9
  48.6 3.8 %collective-permute-start.9 = (bf16[32,32,128]{2,1,0:T(8,128)(2,1)S(1)}, bf16[32,32,128]{2,1,0:T(8,128)(2,1)S(1)}, u32[]{:S(2)}, u32[]{:S(2)}) collective-permute-start(bf16[32,32,128]{2,1,0:T(8,128)(2,1)S(1)} %get-tuple-element.15), channel_id=1, source_target_pairs={{0,160},{32,128},{64,224},{96,192},{128,32},{160,0},{192,96},{224,... | collective-permute-start | bytes 786440 | tf_op jit(solution)/shard_map/ppermute | solution.py:9
  52.6 2.5 %collective-permute-start.10 = (bf16[32,32,128]{2,1,0:T(8,128)(2,1)S(1)}, bf16[32,32,128]{2,1,0:T(8,128)(2,1)S(1)}, u32[]{:S(2)}, u32[]{:S(2)}) collective-permute-start(bf16[32,32,128]{2,1,0:T(8,128)(2,1)S(1)} %get-tuple-element.14), channel_id=1, source_target_pairs={{0,192},{32,224},{64,128},{96,160},{128,64},{160,96},{192,0},{224,... | collective-permute-start | bytes 786440 | tf_op jit(solution)/shard_map/ppermute | solution.py:9
  55.1 1.6 %convolution_bitcast_fusion.6 = bf16[32,32,128]{2,0,1:T(8,128)(2,1)S(1)} fusion(bf16[32,32,128]{2,1,0:T(8,128)(2,1)S(1)} %collective-permute-done.5, bf16[256,128,128]{2,1,0:T(8,128)(2,1)} %param.8, s32[]{:T(128)S(6)} %select_n.231), kind=kOutput, calls=%fused_computation.23 | convolution fusion | flops 33554432 | bytes 1572868 | tf_op jit(solution)/shard_map/sfj,sji->fsi/dot_general | solution.py:54
  57.1 2.8 %collective-permute-start.11 = (bf16[32,32,128]{2,1,0:T(8,128)(2,1)S(1)}, bf16[32,32,128]{2,1,0:T(8,128)(2,1)S(1)}, u32[]{:S(2)}, u32[]{:S(2)}) collective-permute-start(bf16[32,32,128]{2,1,0:T(8,128)(2,1)S(1)} %get-tuple-element.13), channel_id=1, source_target_pairs={{0,224},{32,192},{64,160},{96,128},{128,96},{160,64},{192,32},{224... | collective-permute-start | bytes 786440 | tf_op jit(solution)/shard_map/ppermute | solution.py:9
  59.9 1.6 %convolution_bitcast_fusion.5 = bf16[32,32,128]{2,0,1:T(8,128)(2,1)S(1)} fusion(bf16[32,32,128]{2,1,0:T(8,128)(2,1)S(1)} %collective-permute-done.6, bf16[256,128,128]{2,1,0:T(8,128)(2,1)} %param.8, s32[]{:T(128)S(6)} %select_n.241), kind=kOutput, calls=%fused_computation.22 | convolution fusion | flops 33554432 | bytes 1572868 | tf_op jit(solution)/shard_map/sfj,sji->fsi/dot_general | solution.py:54
  64.1 1.4 %collective-permute-done.10 = bf16[32,32,128]{2,1,0:T(8,128)(2,1)S(1)} collective-permute-done((bf16[32,32,128]{2,1,0:T(8,128)(2,1)S(1)}, bf16[32,32,128]{2,1,0:T(8,128)(2,1)S(1)}, u32[]{:S(2)}, u32[]{:S(2)}) %collective-permute-start.10) | collective-permute-done | bytes 262176 | tf_op jit(solution)/shard_map/ppermute | solution.py:9
  66.3 3.9 %collective-permute-done.3 = bf16[8,32,1024]{2,1,0:T(8,128)(2,1)S(1)} collective-permute-done((bf16[8,32,1024]{2,1,0:T(8,128)(2,1)S(1)}, bf16[8,32,1024]{2,1,0:T(8,128)(2,1)S(1)}, u32[]{:S(2)}, u32[]{:S(2)}) %collective-permute-start.3) | collective-permute-done | bytes 524320 | tf_op jit(solution)/shard_map/ppermute | solution.py:9
  70.5 11.3 %collective-permute-start.4 = (bf16[16,32,1024]{2,1,0:T(8,128)(2,1)S(1)}, bf16[16,32,1024]{2,1,0:T(8,128)(2,1)}, u32[]{:S(2)}, u32[]{:S(2)}) collective-permute-start(bf16[16,32,1024]{2,1,0:T(8,128)(2,1)S(1)} %bitcast.127), channel_id=1, source_target_pairs={{0,1},{1,0},{2,3},{3,2},{4,5},{5,4},{6,7},{7,6},{8,9},{9,8},{10,11... | collective-permute-start | bytes 3145736 | tf_op jit(solution)/shard_map/ppermute | solution.py:9
  84.2 3.7 %all-to-all-start.1 = ((bf16[32,32,256]{2,0,1:T(8,128)(2,1)}), bf16[32,32,256]{2,0,1:T(8,128)(2,1)S(1)}, u32[]{:S(2)}, u32[]{:S(2)}) async-start(bf16[32,32,256]{2,0,1:T(8,128)(2,1)} %copy.58), calls=%async_computation.1 | async-start | bytes 1048576 | tf_op jit(solution)/shard_map/all_to_all | solution.py:69
  89.6 14.8 %all-to-all-done.1 = bf16[32,32,256]{2,0,1:T(8,128)(2,1)S(1)} async-done(((bf16[32,32,256]{2,0,1:T(8,128)(2,1)}), bf16[32,32,256]{2,0,1:T(8,128)(2,1)S(1)}, u32[]{:S(2)}, u32[]{:S(2)}) %all-to-all-start.1) | async-done | bytes 524320 | tf_op jit(solution)/shard_map/all_to_all | solution.py:69
  105.2 21.4 %all_to_all.47 = bf16[32,32,256]{2,1,0:T(8,128)(2,1)S(1)} all-to-all(bf16[32,32,256]{2,1,0:T(8,128)(2,1)S(1)} %bitcast.134), channel_id=1, replica_groups=mesh['row'=8,'feat'=32] {'feat'}, dimensions={0} | all-to-all | bytes 1048576 | tf_op jit(solution)/shard_map/all_to_all | solution.py:72
  (75 shorter events, 17.7 us)
Async XLA Ops:
  0.0 9.8 %copy-start = (bf16[32,8192]{1,0:T(8,128)(2,1)S(1)}, bf16[32,8192]{1,0:T(8,128)(2,1)}, u32[]{:S(2)}) copy-start(bf16[32,8192]{1,0:T(8,128)(2,1)} %param.7) | copy-start | bytes 1572868
  0.0 22.0 %collective-permute-start = (bf16[1,32,1024]{2,1,0:T(8,128)(2,1)}, bf16[1,32,1024]{2,1,0:T(8,128)(2,1)S(1)}, u32[]{:S(2)}, u32[]{:S(2)}) collective-permute-start(bf16[1,32,1024]{2,1,0:T(8,128)(2,1)} %bitcast.136), channel_id=1, source_target_pairs={{0,16},{1,17},{2,18},{3,19},{4,20},{5,21},{6,22},{7,23},{8,24},{9,... | collective-permute-start | bytes 196616 | tf_op jit(solution)/shard_map/ppermute | solution.py:9
  3.4 29.0 %all-to-all-start = ((s32[8,1,32]{2,1,0:T(1,128)}), s32[8,1,32]{2,1,0:T(1,128)S(1)}, u32[]{:S(2)}, u32[]{:S(2)}) async-start(s32[8,1,32]{2,1,0:T(1,128)} %all_to_all.34), calls=%async_computation | async-start | bytes 8192 | tf_op jit(solution)/shard_map/all_to_all | solution.py:40
  22.8 9.5 %collective-permute-start.1 = (bf16[2,32,1024]{2,1,0:T(8,128)(2,1)S(1)}, bf16[2,32,1024]{2,1,0:T(8,128)(2,1)S(1)}, u32[]{:S(2)}, u32[]{:S(2)}) collective-permute-start(bf16[2,32,1024]{2,1,0:T(8,128)(2,1)S(1)} %maximum_bitcast_fusion), channel_id=1, source_target_pairs={{0,8},{1,9},{2,10},{3,11},{4,12},{5,13},{6,14},{7,15},{8,0},{9,1},... | collective-permute-start | bytes 393224 | tf_op jit(solution)/shard_map/ppermute | solution.py:9
  34.1 22.6 %copy-start.1 = (f32[64,32,128]{2,0,1:T(8,128)S(1)}, f32[64,32,128]{2,0,1:T(8,128)}, u32[]{:S(2)}) copy-start(f32[64,32,128]{2,0,1:T(8,128)} %fusion.19) | copy-start | bytes 3145732
  34.2 28.0 %slice-start = ((s8[8388608]{0:T(1024)(128)(4,1)}), s8[4194304]{0:T(1024)(128)(4,1)S(1)}, s32[]{:S(2)}) async-start(s8[8388608]{0:T(1024)(128)(4,1)} %bitcast.125), calls=%async_computation.3 | async-start | bytes 8388608
  34.2 14.5 %collective-permute-start.2 = (bf16[4,32,1024]{2,1,0:T(8,128)(2,1)S(1)}, bf16[4,32,1024]{2,1,0:T(8,128)(2,1)S(1)}, u32[]{:S(2)}, u32[]{:S(2)}) collective-permute-start(bf16[4,32,1024]{2,1,0:T(8,128)(2,1)S(1)} %bitcast.131), channel_id=1, source_target_pairs={{0,4},{1,5},{2,6},{3,7},{4,0},{5,1},{6,2},{7,3},{8,12},{9,13},{10,... | collective-permute-start | bytes 786440 | tf_op jit(solution)/shard_map/ppermute | solution.py:9
  40.0 12.6 %collective-permute-start.5 = (bf16[32,32,128]{2,1,0:T(8,128)(2,1)S(1)}, bf16[32,32,128]{2,1,0:T(8,128)(2,1)S(1)}, u32[]{:S(2)}, u32[]{:S(2)}) collective-permute-start(bf16[32,32,128]{2,1,0:T(8,128)(2,1)S(1)} %get-tuple-element.19), channel_id=1, source_target_pairs={{0,32},{32,0},{64,96},{96,64},{128,160},{160,128},{192,224},{224,1... | collective-permute-start | bytes 786440 | tf_op jit(solution)/shard_map/ppermute | solution.py:9
  41.6 15.5 %collective-permute-start.6 = (bf16[32,32,128]{2,1,0:T(8,128)(2,1)S(1)}, bf16[32,32,128]{2,1,0:T(8,128)(2,1)S(1)}, u32[]{:S(2)}, u32[]{:S(2)}) collective-permute-start(bf16[32,32,128]{2,1,0:T(8,128)(2,1)S(1)} %get-tuple-element.18), channel_id=1, source_target_pairs={{0,64},{32,96},{64,0},{96,32},{128,192},{160,224},{192,128},{224,1... | collective-permute-start | bytes 786440 | tf_op jit(solution)/shard_map/ppermute | solution.py:9
  44.0 17.9 %collective-permute-start.7 = (bf16[32,32,128]{2,1,0:T(8,128)(2,1)S(1)}, bf16[32,32,128]{2,1,0:T(8,128)(2,1)S(1)}, u32[]{:S(2)}, u32[]{:S(2)}) collective-permute-start(bf16[32,32,128]{2,1,0:T(8,128)(2,1)S(1)} %get-tuple-element.17), channel_id=1, source_target_pairs={{0,96},{32,64},{64,32},{96,0},{128,224},{160,192},{192,160},{224,1... | collective-permute-start | bytes 786440 | tf_op jit(solution)/shard_map/ppermute | solution.py:9
  44.1 18.9 %collective-permute-start.8 = (bf16[32,32,128]{2,1,0:T(8,128)(2,1)S(1)}, bf16[32,32,128]{2,1,0:T(8,128)(2,1)S(1)}, u32[]{:S(2)}, u32[]{:S(2)}) collective-permute-start(bf16[32,32,128]{2,1,0:T(8,128)(2,1)S(1)} %get-tuple-element.16), channel_id=1, source_target_pairs={{0,128},{32,160},{64,192},{96,224},{128,0},{160,32},{192,64},{224,... | collective-permute-start | bytes 786440 | tf_op jit(solution)/shard_map/ppermute | solution.py:9
  48.6 15.1 %collective-permute-start.9 = (bf16[32,32,128]{2,1,0:T(8,128)(2,1)S(1)}, bf16[32,32,128]{2,1,0:T(8,128)(2,1)S(1)}, u32[]{:S(2)}, u32[]{:S(2)}) collective-permute-start(bf16[32,32,128]{2,1,0:T(8,128)(2,1)S(1)} %get-tuple-element.15), channel_id=1, source_target_pairs={{0,160},{32,128},{64,224},{96,192},{128,32},{160,0},{192,96},{224,... | collective-permute-start | bytes 786440 | tf_op jit(solution)/shard_map/ppermute | solution.py:9
  52.5 9.7 %slice-start.1 = ((s8[8388608]{0:T(1024)(128)(4,1)}), s8[4194304]{0:T(1024)(128)(4,1)S(1)}, s32[]{:S(2)}) async-start(s8[8388608]{0:T(1024)(128)(4,1)} %bitcast.125), calls=%async_computation.4 | async-start | bytes 8388608
  52.6 12.9 %collective-permute-start.10 = (bf16[32,32,128]{2,1,0:T(8,128)(2,1)S(1)}, bf16[32,32,128]{2,1,0:T(8,128)(2,1)S(1)}, u32[]{:S(2)}, u32[]{:S(2)}) collective-permute-start(bf16[32,32,128]{2,1,0:T(8,128)(2,1)S(1)} %get-tuple-element.14), channel_id=1, source_target_pairs={{0,192},{32,224},{64,128},{96,160},{128,64},{160,96},{192,0},{224,... | collective-permute-start | bytes 786440 | tf_op jit(solution)/shard_map/ppermute | solution.py:9
  57.1 25.0 %collective-permute-start.11 = (bf16[32,32,128]{2,1,0:T(8,128)(2,1)S(1)}, bf16[32,32,128]{2,1,0:T(8,128)(2,1)S(1)}, u32[]{:S(2)}, u32[]{:S(2)}) collective-permute-start(bf16[32,32,128]{2,1,0:T(8,128)(2,1)S(1)} %get-tuple-element.13), channel_id=1, source_target_pairs={{0,224},{32,192},{64,160},{96,128},{128,96},{160,64},{192,32},{224... | collective-permute-start | bytes 786440 | tf_op jit(solution)/shard_map/ppermute | solution.py:9
  61.9 8.3 %collective-permute-start.3 = (bf16[8,32,1024]{2,1,0:T(8,128)(2,1)S(1)}, bf16[8,32,1024]{2,1,0:T(8,128)(2,1)S(1)}, u32[]{:S(2)}, u32[]{:S(2)}) collective-permute-start(bf16[8,32,1024]{2,1,0:T(8,128)(2,1)S(1)} %bitcast.128), channel_id=1, source_target_pairs={{0,2},{1,3},{2,0},{3,1},{4,6},{5,7},{6,4},{7,5},{8,10},{9,11},{10,... | collective-permute-start | bytes 1572872 | tf_op jit(solution)/shard_map/ppermute | solution.py:9
  70.5 17.4 %collective-permute-start.4 = (bf16[16,32,1024]{2,1,0:T(8,128)(2,1)S(1)}, bf16[16,32,1024]{2,1,0:T(8,128)(2,1)}, u32[]{:S(2)}, u32[]{:S(2)}) collective-permute-start(bf16[16,32,1024]{2,1,0:T(8,128)(2,1)S(1)} %bitcast.127), channel_id=1, source_target_pairs={{0,1},{1,0},{2,3},{3,2},{4,5},{5,4},{6,7},{7,6},{8,9},{9,8},{10,11... | collective-permute-start | bytes 3145736 | tf_op jit(solution)/shard_map/ppermute | solution.py:9
  82.5 21.9 %copy-start.2 = (f32[1024]{0:T(1024)S(1)}, f32[1024]{0:T(1024)}, u32[]{:S(2)}) copy-start(f32[1024]{0:T(1024)} %param.13) | copy-start | bytes 12292
  84.2 20.3 %all-to-all-start.1 = ((bf16[32,32,256]{2,0,1:T(8,128)(2,1)}), bf16[32,32,256]{2,0,1:T(8,128)(2,1)S(1)}, u32[]{:S(2)}, u32[]{:S(2)}) async-start(bf16[32,32,256]{2,0,1:T(8,128)(2,1)} %copy.58), calls=%async_computation.1 | async-start | bytes 1048576 | tf_op jit(solution)/shard_map/all_to_all | solution.py:69

commit v4 on v2

--- a/solution.py
+++ b/solution.py
@@ -55,12 +55,14 @@
     picked_all = jnp.take(blocks_t, send_cols, axis=0).reshape(
         cycle_len - 1, slot_total, feat_width, tile_size
     )
-    held = [swap_with(picked_all[m - 1], "row", m) for m in range(1, cycle_len)]
+    held = {}
+    for m in range(1, cycle_len):
+        held[m] = swap_with(picked_all[m - 1], "row", m)
     own_cols = lax.dynamic_slice_in_dim(tile_col, own_row * slot_total, slot_total, 0)
     running = jnp.zeros((feat_width, row_blocks, tile_size), jnp.float32)
     running = add_source(running, jnp.take(blocks_t, own_cols, axis=0), own_row)
     for step_num in range(1, cycle_len):
-        running = add_source(running, held[step_num - 1], jnp.bitwise_xor(own_row, step_num))
+        running = add_source(running, held[step_num], jnp.bitwise_xor(own_row, step_num))
     aggregated = running.reshape(feat_width, rows_here).astype(jnp.bfloat16)
     agg_t = lax.all_to_all(aggregated, "feat", 1, 0, tiled=True)
     pre_act = jnp.dot(w_full, agg_t, preferred_element_type=jnp.float32)

time: 132 us -> 132 us (level)
  no operation moved by 1% of the time
where the time goes in v4:
time: 132 us; the launch traced here: 130 us
  starting transfers between devices  47.8 us (36%)
  waiting for transfers between devices  31.5 us (24%)
  blocking collectives  21.4 us (16%)
  matrix products  11.4 us (9%)
  local copies, waits for them, and re-layouts  9 us (7%)
  other arithmetic  8.31 us (6%)
    ppermute x12, starting transfers between devices, swap_with(): return lax.ppermute(value, axis, [(i, i ^ mask) for i in range(count)])  34.4 us
    all_to_all x1, blocking collectives, on_device(): activated = lax.all_to_all(act_t, 'feat', 0, 1, tiled=True)  21.4 us
    ppermute x12, waiting for transfers between devices, swap_with(): return lax.ppermute(value, axis, [(i, i ^ mask) for i in range(count)])  16.7 us
    all_to_all x1, waiting for transfers between devices, on_device(): agg_t = lax.all_to_all(aggregated, 'feat', 1, 0, tiled=True)  14.8 us
    all_to_all x1, starting transfers between devices, on_device(): lax.all_to_all(tile_col.reshape(cycle_len, slot_total), 'row', 0, 0, tile...  7.47 us
    dot_general x8, matrix products, add_source(): jnp.einsum('sfj,sji->fsi', picked, tiles_part, preferred_element_type=jnp...  6.74 us
    all_to_all x1, starting transfers between devices, on_device(): agg_t = lax.all_to_all(aggregated, 'feat', 1, 0, tiled=True)  5.93 us
    gather x3, other arithmetic, on_device(): live_all = tile_ids % slot_total < counts_here[tile_ids // slot_total]  5.01 us
  transfers between devices with their start and end apart: 14, of which 3 were waited for; matrix products, arithmetic and copies ran while one was open for 20% of the time, Pallas kernels for 0%

profile of v4, /device:TPU:1, one launch (start us, length us, event | category | flops | bytes accessed | tf_op | source)
XLA Modules:
  0.0 129.9 jit_solution(4840599006395470233)
XLA Ops:
  0.0 1.4 %all_to_all.34 = s32[8,1,32]{2,1,0:T(1,128)} reshape(s32[256]{0:T(256)} %param.10) | data formatting | bytes 2048 | tf_op jit(solution)/shard_map/all_to_all | solution.py:38
  1.4 7.5 %all-to-all-start = ((s32[8,1,32]{2,1,0:T(1,128)}), s32[8,1,32]{2,1,0:T(1,128)S(1)}, u32[]{:S(2)}, u32[]{:S(2)}) async-start(s32[8,1,32]{2,1,0:T(1,128)} %all_to_all.34), calls=%async_computation | async-start | bytes 8192 | tf_op jit(solution)/shard_map/all_to_all | solution.py:38
  10.2 1.6 %fusion.64 = (s32[1,1]{1,0:T(1,128)}, s32[1,1]{1,0:T(1,128)}, s32[1,1]{1,0:T(1,128)}, s32[1,1]{1,0:T(1,128)}, s32[1,1]{1,0:T(1,128)}, /*index=5*/s32[1,1]{1,0:T(1,128)}, s32[1,1]{1,0:T(1,128)}, s32[1,1]{1,0:T(1,128)}) fusion(s32[1,8]{1,0:T(1,128)} %param.11), kind=kLoop, calls=%fused_computation.128 | loop fusion | bytes 64 | tf_op jit(solution)/shard_map/gather | solution.py:42
  11.8 4.3 %compare_select_fusion.2 = s32[256,1]{0,1:T(1,128)S(1)} fusion(s32[]{:T(128)} %bitcast.18, s32[]{:T(128)} %bitcast.19, s32[]{:T(128)} %bitcast.20, s32[]{:T(128)} %bitcast.21, s32[]{:T(128)} %bitcast.22, s32[]{:T(128)} %bitcast.24, s32[]{:T(128)} %bitcast.23), kind=kLoop, calls=%fused_computation.106 | loop fusion | flops 5888 | bytes 1052 | tf_op jit(solution)/shard_map/gather | solution.py:42
  18.4 1.7 %convolution_bitcast_fusion.7 = bf16[32,32,128]{2,0,1:T(8,128)(2,1)S(1)} fusion(bf16[256,128,128]{2,1,0:T(8,128)(2,1)} %param.8, s32[]{:T(128)S(6)} %select_n.227, bf16[32,32,128]{2,1,0:T(8,128)(2,1)S(1)} %gather_fusion, pred[32]{0:T(512)(128)(4,1)S(1)} %get-tuple-element.5), kind=kOutput, calls=%fused_computation.24 | convolution fusion | flops 33685504 | bytes 1572900 | tf_op jit(solution)/shard_map/sfj,sji->fsi/dot_general | solution.py:50
  20.1 1.4 %fusion.19 = f32[64,32,128]{2,0,1:T(8,128)} fusion(bf16[32,32,128]{2,0,1:T(8,128)(2,1)S(1)} %convolution_bitcast_fusion.7, pred[8,32,64]{2,1,0:T(32,128)(4,1)S(1)} %fusion.24, s32[]{:T(128)S(6)} %select_n.226), kind=kOutput, calls=%fused_computation.45 | convolution fusion | flops 16777216 | bytes 1314820 | tf_op jit(solution)/shard_map/fsi,sr->fri/dot_general | solution.py:51
  22.3 1.0 gather_fusion.2
  23.7 7.0 %collective-permute-start.1 = (bf16[2,32,1024]{2,1,0:T(8,128)(2,1)S(1)}, bf16[2,32,1024]{2,1,0:T(8,128)(2,1)S(1)}, u32[]{:S(2)}, u32[]{:S(2)}) collective-permute-start(bf16[2,32,1024]{2,1,0:T(8,128)(2,1)S(1)} %maximum_bitcast_fusion), channel_id=1, source_target_pairs={{0,8},{1,9},{2,10},{3,11},{4,12},{5,13},{6,14},{7,15},{8,0},{9,1},... | collective-permute-start | bytes 393224 | tf_op jit(solution)/shard_map/ppermute | solution.py:9
  31.0 1.6 %collective-permute-start.5 = (bf16[32,32,128]{2,1,0:T(8,128)(2,1)S(1)}, bf16[32,32,128]{2,1,0:T(8,128)(2,1)S(1)}, u32[]{:S(2)}, u32[]{:S(2)}) collective-permute-start(bf16[32,32,128]{2,1,0:T(8,128)(2,1)S(1)} %get-tuple-element.15), channel_id=1, source_target_pairs={{0,32},{32,0},{64,96},{96,64},{128,160},{160,128},{192,224},{224,1... | collective-permute-start | bytes 786440 | tf_op jit(solution)/shard_map/ppermute | solution.py:9
  32.5 2.4 %collective-permute-start.6 = (bf16[32,32,128]{2,1,0:T(8,128)(2,1)S(1)}, bf16[32,32,128]{2,1,0:T(8,128)(2,1)S(1)}, u32[]{:S(2)}, u32[]{:S(2)}) collective-permute-start(bf16[32,32,128]{2,1,0:T(8,128)(2,1)S(1)} %get-tuple-element.14), channel_id=1, source_target_pairs={{0,64},{32,96},{64,0},{96,32},{128,192},{160,224},{192,128},{224,1... | collective-permute-start | bytes 786440 | tf_op jit(solution)/shard_map/ppermute | solution.py:9
  35.0 3.5 %collective-permute-start.8 = (bf16[32,32,128]{2,1,0:T(8,128)(2,1)S(1)}, bf16[32,32,128]{2,1,0:T(8,128)(2,1)S(1)}, u32[]{:S(2)}, u32[]{:S(2)}) collective-permute-start(bf16[32,32,128]{2,1,0:T(8,128)(2,1)S(1)} %get-tuple-element.12), channel_id=1, source_target_pairs={{0,128},{32,160},{64,192},{96,224},{128,0},{160,32},{192,64},{224,... | collective-permute-start | bytes 786440 | tf_op jit(solution)/shard_map/ppermute | solution.py:9
  38.6 6.1 %collective-permute-start.10 = (bf16[32,32,128]{2,1,0:T(8,128)(2,1)S(1)}, bf16[32,32,128]{2,1,0:T(8,128)(2,1)S(1)}, u32[]{:S(2)}, u32[]{:S(2)}) collective-permute-start(bf16[32,32,128]{2,1,0:T(8,128)(2,1)S(1)} %get-tuple-element.10), channel_id=1, source_target_pairs={{0,192},{32,224},{64,128},{96,160},{128,64},{160,96},{192,0},{224,... | collective-permute-start | bytes 786440 | tf_op jit(solution)/shard_map/ppermute | solution.py:9
  44.7 1.6 %convolution_bitcast_fusion.6 = bf16[32,32,128]{2,0,1:T(8,128)(2,1)S(1)} fusion(bf16[32,32,128]{2,1,0:T(8,128)(2,1)S(1)} %collective-permute-done.5, bf16[256,128,128]{2,1,0:T(8,128)(2,1)} %param.8, s32[]{:T(128)S(6)} %select_n.231), kind=kOutput, calls=%fused_computation.23 | convolution fusion | flops 33554432 | bytes 1572868 | tf_op jit(solution)/shard_map/sfj,sji->fsi/dot_general | solution.py:50
  46.7 3.2 %collective-permute-start.11 = (bf16[32,32,128]{2,1,0:T(8,128)(2,1)S(1)}, bf16[32,32,128]{2,1,0:T(8,128)(2,1)S(1)}, u32[]{:S(2)}, u32[]{:S(2)}) collective-permute-start(bf16[32,32,128]{2,1,0:T(8,128)(2,1)S(1)} %get-tuple-element.9), channel_id=1, source_target_pairs={{0,224},{32,192},{64,160},{96,128},{128,96},{160,64},{192,32},{224... | collective-permute-start | bytes 786440 | tf_op jit(solution)/shard_map/ppermute | solution.py:9
  49.8 1.6 %convolution_bitcast_fusion.5 = bf16[32,32,128]{2,0,1:T(8,128)(2,1)S(1)} fusion(bf16[32,32,128]{2,1,0:T(8,128)(2,1)S(1)} %collective-permute-done.6, bf16[256,128,128]{2,1,0:T(8,128)(2,1)} %param.8, s32[]{:T(128)S(6)} %select_n.241), kind=kOutput, calls=%fused_computation.22 | convolution fusion | flops 33554432 | bytes 1572868 | tf_op jit(solution)/shard_map/sfj,sji->fsi/dot_general | solution.py:50
  53.8 7.0 %collective-permute-done.2 = bf16[4,32,1024]{2,1,0:T(8,128)(2,1)S(1)} collective-permute-done((bf16[4,32,1024]{2,1,0:T(8,128)(2,1)S(1)}, bf16[4,32,1024]{2,1,0:T(8,128)(2,1)S(1)}, u32[]{:S(2)}, u32[]{:S(2)}) %collective-permute-start.2) | collective-permute-done | bytes 262176 | tf_op jit(solution)/shard_map/ppermute | solution.py:9
  62.5 9.7 %collective-permute-done.3 = bf16[8,32,1024]{2,1,0:T(8,128)(2,1)S(1)} collective-permute-done((bf16[8,32,1024]{2,1,0:T(8,128)(2,1)S(1)}, bf16[8,32,1024]{2,1,0:T(8,128)(2,1)S(1)}, u32[]{:S(2)}, u32[]{:S(2)}) %collective-permute-start.3) | collective-permute-done | bytes 524320 | tf_op jit(solution)/shard_map/ppermute | solution.py:9
  72.4 9.6 %collective-permute-start.4 = (bf16[16,32,1024]{2,1,0:T(8,128)(2,1)S(1)}, bf16[16,32,1024]{2,1,0:T(8,128)(2,1)}, u32[]{:S(2)}, u32[]{:S(2)}) collective-permute-start(bf16[16,32,1024]{2,1,0:T(8,128)(2,1)S(1)} %bitcast.129), channel_id=1, source_target_pairs={{0,1},{1,0},{2,3},{3,2},{4,5},{5,4},{6,7},{7,6},{8,9},{9,8},{10,11... | collective-permute-start | bytes 3145736 | tf_op jit(solution)/shard_map/ppermute | solution.py:9
  83.4 1.1 copy.58
  84.5 5.9 %all-to-all-start.1 = ((bf16[32,32,256]{2,0,1:T(8,128)(2,1)}), bf16[32,32,256]{2,0,1:T(8,128)(2,1)S(1)}, u32[]{:S(2)}, u32[]{:S(2)}) async-start(bf16[32,32,256]{2,0,1:T(8,128)(2,1)} %copy.58), calls=%async_computation.1 | async-start | bytes 1048576 | tf_op jit(solution)/shard_map/all_to_all | solution.py:67
  90.4 1.4 %select_bitcast_fusion.1 = (bf16[16,1,32,1024]{3,2,0,1:T(8,128)(2,1)S(1)}, bf16[16,1,32,1024]{3,2,0,1:T(8,128)(2,1)S(1)}) fusion(bf16[16,32,1024]{2,1,0:T(8,128)(2,1)} %collective-permute-done.4, pred[]{:T(512)S(6)} %eq.33, bf16[8,2,32,1024]{3,2,1,0:T(8,128)(2,1)S(1)} %copy.47), kind=kLoop, calls=%fused_computation.35 | loop fusion | flops 1048576 | bytes 4194305 | tf_op jit(solution)/shard_map/stack | solution.py:23
  92.2 14.8 %all-to-all-done.1 = bf16[32,32,256]{2,0,1:T(8,128)(2,1)S(1)} async-done(((bf16[32,32,256]{2,0,1:T(8,128)(2,1)}), bf16[32,32,256]{2,0,1:T(8,128)(2,1)S(1)}, u32[]{:S(2)}, u32[]{:S(2)}) %all-to-all-start.1) | async-done | bytes 524320 | tf_op jit(solution)/shard_map/all_to_all | solution.py:67
  107.7 21.4 %all_to_all.47 = bf16[32,32,256]{2,1,0:T(8,128)(2,1)S(1)} all-to-all(bf16[32,32,256]{2,1,0:T(8,128)(2,1)S(1)} %bitcast.135), channel_id=1, replica_groups=mesh['row'=8,'feat'=32] {'feat'}, dimensions={0} | all-to-all | bytes 1048576 | tf_op jit(solution)/shard_map/all_to_all | solution.py:70
  129.1 0.8 copy.61
  (77 shorter events, 12.0 us)
Async XLA Ops:
  0.0 10.1 %copy-start = (bf16[32,8192]{1,0:T(8,128)(2,1)S(1)}, bf16[32,8192]{1,0:T(8,128)(2,1)}, u32[]{:S(2)}) copy-start(bf16[32,8192]{1,0:T(8,128)(2,1)} %param.7) | copy-start | bytes 1572868
  0.0 23.6 %copy-start.2 = (bf16[32,1024]{1,0:T(8,128)(2,1)S(1)}, bf16[32,1024]{1,0:T(8,128)(2,1)}, u32[]{:S(2)}) copy-start(bf16[32,1024]{1,0:T(8,128)(2,1)} %param.12) | copy-start | bytes 196612
  1.4 20.1 %all-to-all-start = ((s32[8,1,32]{2,1,0:T(1,128)}), s32[8,1,32]{2,1,0:T(1,128)S(1)}, u32[]{:S(2)}, u32[]{:S(2)}) async-start(s32[8,1,32]{2,1,0:T(1,128)} %all_to_all.34), calls=%async_computation | async-start | bytes 8192 | tf_op jit(solution)/shard_map/all_to_all | solution.py:38
  8.9 14.7 %collective-permute-start = (bf16[1,32,1024]{2,1,0:T(8,128)(2,1)}, bf16[1,32,1024]{2,1,0:T(8,128)(2,1)S(1)}, u32[]{:S(2)}, u32[]{:S(2)}) collective-permute-start(bf16[1,32,1024]{2,1,0:T(8,128)(2,1)} %bitcast.137), channel_id=1, source_target_pairs={{0,16},{1,17},{2,18},{3,19},{4,20},{5,21},{6,22},{7,23},{8,24},{9,... | collective-permute-start | bytes 196616 | tf_op jit(solution)/shard_map/ppermute | solution.py:9
  23.2 23.0 %copy-start.1 = (f32[64,32,128]{2,0,1:T(8,128)S(1)}, f32[64,32,128]{2,0,1:T(8,128)}, u32[]{:S(2)}) copy-start(f32[64,32,128]{2,0,1:T(8,128)} %fusion.19) | copy-start | bytes 3145732
  23.3 29.0 %slice-start = ((s8[8388608]{0:T(1024)(128)(4,1)}), s8[4194304]{0:T(1024)(128)(4,1)S(1)}, s32[]{:S(2)}) async-start(s8[8388608]{0:T(1024)(128)(4,1)} %bitcast.127), calls=%async_computation.3 | async-start | bytes 8388608
  23.7 14.9 %collective-permute-start.1 = (bf16[2,32,1024]{2,1,0:T(8,128)(2,1)S(1)}, bf16[2,32,1024]{2,1,0:T(8,128)(2,1)S(1)}, u32[]{:S(2)}, u32[]{:S(2)}) collective-permute-start(bf16[2,32,1024]{2,1,0:T(8,128)(2,1)S(1)} %maximum_bitcast_fusion), channel_id=1, source_target_pairs={{0,8},{1,9},{2,10},{3,11},{4,12},{5,13},{6,14},{7,15},{8,0},{9,1},... | collective-permute-start | bytes 393224 | tf_op jit(solution)/shard_map/ppermute | solution.py:9
  31.0 7.6 %collective-permute-start.5 = (bf16[32,32,128]{2,1,0:T(8,128)(2,1)S(1)}, bf16[32,32,128]{2,1,0:T(8,128)(2,1)S(1)}, u32[]{:S(2)}, u32[]{:S(2)}) collective-permute-start(bf16[32,32,128]{2,1,0:T(8,128)(2,1)S(1)} %get-tuple-element.15), channel_id=1, source_target_pairs={{0,32},{32,0},{64,96},{96,64},{128,160},{160,128},{192,224},{224,1... | collective-permute-start | bytes 786440 | tf_op jit(solution)/shard_map/ppermute | solution.py:9
  32.5 14.1 %collective-permute-start.6 = (bf16[32,32,128]{2,1,0:T(8,128)(2,1)S(1)}, bf16[32,32,128]{2,1,0:T(8,128)(2,1)S(1)}, u32[]{:S(2)}, u32[]{:S(2)}) collective-permute-start(bf16[32,32,128]{2,1,0:T(8,128)(2,1)S(1)} %get-tuple-element.14), channel_id=1, source_target_pairs={{0,64},{32,96},{64,0},{96,32},{128,192},{160,224},{192,128},{224,1... | collective-permute-start | bytes 786440 | tf_op jit(solution)/shard_map/ppermute | solution.py:9
  34.9 16.9 %collective-permute-start.7 = (bf16[32,32,128]{2,1,0:T(8,128)(2,1)S(1)}, bf16[32,32,128]{2,1,0:T(8,128)(2,1)S(1)}, u32[]{:S(2)}, u32[]{:S(2)}) collective-permute-start(bf16[32,32,128]{2,1,0:T(8,128)(2,1)S(1)} %get-tuple-element.13), channel_id=1, source_target_pairs={{0,96},{32,64},{64,32},{96,0},{128,224},{160,192},{192,160},{224,1... | collective-permute-start | bytes 786440 | tf_op jit(solution)/shard_map/ppermute | solution.py:9
  35.0 18.0 %collective-permute-start.8 = (bf16[32,32,128]{2,1,0:T(8,128)(2,1)S(1)}, bf16[32,32,128]{2,1,0:T(8,128)(2,1)S(1)}, u32[]{:S(2)}, u32[]{:S(2)}) collective-permute-start(bf16[32,32,128]{2,1,0:T(8,128)(2,1)S(1)} %get-tuple-element.12), channel_id=1, source_target_pairs={{0,128},{32,160},{64,192},{96,224},{128,0},{160,32},{192,64},{224,... | collective-permute-start | bytes 786440 | tf_op jit(solution)/shard_map/ppermute | solution.py:9
  38.5 22.8 %collective-permute-start.9 = (bf16[32,32,128]{2,1,0:T(8,128)(2,1)S(1)}, bf16[32,32,128]{2,1,0:T(8,128)(2,1)S(1)}, u32[]{:S(2)}, u32[]{:S(2)}) collective-permute-start(bf16[32,32,128]{2,1,0:T(8,128)(2,1)S(1)} %get-tuple-element.11), channel_id=1, source_target_pairs={{0,160},{32,128},{64,224},{96,192},{128,32},{160,0},{192,96},{224,... | collective-permute-start | bytes 786440 | tf_op jit(solution)/shard_map/ppermute | solution.py:9
  38.5 13.8 %slice-start.1 = ((s8[8388608]{0:T(1024)(128)(4,1)}), s8[4194304]{0:T(1024)(128)(4,1)S(1)}, s32[]{:S(2)}) async-start(s8[8388608]{0:T(1024)(128)(4,1)} %bitcast.127), calls=%async_computation.4 | async-start | bytes 8388608
  38.6 23.1 %collective-permute-start.10 = (bf16[32,32,128]{2,1,0:T(8,128)(2,1)S(1)}, bf16[32,32,128]{2,1,0:T(8,128)(2,1)S(1)}, u32[]{:S(2)}, u32[]{:S(2)}) collective-permute-start(bf16[32,32,128]{2,1,0:T(8,128)(2,1)S(1)} %get-tuple-element.10), channel_id=1, source_target_pairs={{0,192},{32,224},{64,128},{96,160},{128,64},{160,96},{192,0},{224,... | collective-permute-start | bytes 786440 | tf_op jit(solution)/shard_map/ppermute | solution.py:9
  46.7 35.8 %collective-permute-start.11 = (bf16[32,32,128]{2,1,0:T(8,128)(2,1)S(1)}, bf16[32,32,128]{2,1,0:T(8,128)(2,1)S(1)}, u32[]{:S(2)}, u32[]{:S(2)}) collective-permute-start(bf16[32,32,128]{2,1,0:T(8,128)(2,1)S(1)} %get-tuple-element.9), channel_id=1, source_target_pairs={{0,224},{32,192},{64,160},{96,128},{128,96},{160,64},{192,32},{224... | collective-permute-start | bytes 786440 | tf_op jit(solution)/shard_map/ppermute | solution.py:9
  51.8 9.0 %collective-permute-start.2 = (bf16[4,32,1024]{2,1,0:T(8,128)(2,1)S(1)}, bf16[4,32,1024]{2,1,0:T(8,128)(2,1)S(1)}, u32[]{:S(2)}, u32[]{:S(2)}) collective-permute-start(bf16[4,32,1024]{2,1,0:T(8,128)(2,1)S(1)} %bitcast.133), channel_id=1, source_target_pairs={{0,4},{1,5},{2,6},{3,7},{4,0},{5,1},{6,2},{7,3},{8,12},{9,13},{10,... | collective-permute-start | bytes 786440 | tf_op jit(solution)/shard_map/ppermute | solution.py:9
  61.0 11.1 %collective-permute-start.3 = (bf16[8,32,1024]{2,1,0:T(8,128)(2,1)S(1)}, bf16[8,32,1024]{2,1,0:T(8,128)(2,1)S(1)}, u32[]{:S(2)}, u32[]{:S(2)}) collective-permute-start(bf16[8,32,1024]{2,1,0:T(8,128)(2,1)S(1)} %bitcast.130), channel_id=1, source_target_pairs={{0,2},{1,3},{2,0},{3,1},{4,6},{5,7},{6,4},{7,5},{8,10},{9,11},{10,... | collective-permute-start | bytes 1572872 | tf_op jit(solution)/shard_map/ppermute | solution.py:9
  72.4 18.0 %collective-permute-start.4 = (bf16[16,32,1024]{2,1,0:T(8,128)(2,1)S(1)}, bf16[16,32,1024]{2,1,0:T(8,128)(2,1)}, u32[]{:S(2)}, u32[]{:S(2)}) collective-permute-start(bf16[16,32,1024]{2,1,0:T(8,128)(2,1)S(1)} %bitcast.129), channel_id=1, source_target_pairs={{0,1},{1,0},{2,3},{3,2},{4,5},{5,4},{6,7},{7,6},{8,9},{9,8},{10,11... | collective-permute-start | bytes 3145736 | tf_op jit(solution)/shard_map/ppermute | solution.py:9
  82.8 24.2 %copy-start.3 = (f32[1024]{0:T(1024)S(1)}, f32[1024]{0:T(1024)}, u32[]{:S(2)}) copy-start(f32[1024]{0:T(1024)} %param.13) | copy-start | bytes 12292
  84.5 22.5 %all-to-all-start.1 = ((bf16[32,32,256]{2,0,1:T(8,128)(2,1)}), bf16[32,32,256]{2,0,1:T(8,128)(2,1)S(1)}, u32[]{:S(2)}, u32[]{:S(2)}) async-start(bf16[32,32,256]{2,0,1:T(8,128)(2,1)} %copy.58), calls=%async_computation.1 | async-start | bytes 1048576 | tf_op jit(solution)/shard_map/all_to_all | solution.py:67

commit v5 on v3

--- a/solution.py
+++ b/solution.py
@@ -36,10 +36,8 @@
     counts_here = tile_count[0]
 
     bits = weight_bits()
-    w_mid = gather_weight(weight.reshape(1, *weight.shape), bits[:2])
+    w_mid = gather_weight(weight.reshape(1, *weight.shape), bits[:-1])
     cols_out = lax.all_to_all(tile_col.reshape(cycle_len, slot_total), "row", 0, 0, tiled=True)
-    w_mid, cols_out = lax.optimization_barrier((w_mid, cols_out))
-    w_full = gather_weight(w_mid, bits[2:]).reshape(-1, weight.shape[1])
     blocks_t = node_features.reshape(feat_width, row_blocks, tile_size).transpose(1, 0, 2)
 
     tile_ids = jnp.arange(cycle_len * slot_total)
@@ -65,6 +63,8 @@
     running = add_source(running, jnp.take(blocks_t, own_cols, axis=0), own_row)
     for step_num in range(1, cycle_len):
         running = add_source(running, held[step_num - 1], jnp.bitwise_xor(own_row, step_num))
+    w_mid, _ = lax.optimization_barrier((w_mid, running))
+    w_full = gather_weight(w_mid, bits[-1:]).reshape(-1, weight.shape[1])
     aggregated = running.reshape(feat_width, rows_here).astype(jnp.bfloat16)
     agg_t = lax.all_to_all(aggregated, "feat", 1, 0, tiled=True)
     pre_act = jnp.dot(w_full, agg_t, preferred_element_type=jnp.float32)

time: 129 us -> 131 us (1.016)
  waiting for transfers between devices: 24.3 us -> 28.8 us
  starting transfers between devices: 51.8 us -> 48.2 us
    ppermute x12, starting transfers between devices: 41.8 us -> 34.8 us  [swap_with(): return lax.ppermute(value, axis, [(i, i ^ mask) for i in range(count)])]
    ppermute x12, waiting for transfers between devices: 9.45 us -> 13.9 us  [swap_with(): return lax.ppermute(value, axis, [(i, i ^ mask) for i in range(count)])]
    all_to_all x1, starting transfers between devices: 3.68 us -> 5.92 us  [on_device(): agg_t = lax.all_to_all(aggregated, 'feat', 1, 0, tiled=True)]
  transfers between devices with their start and end apart: 14 -> 14, of which waited for: 5 -> 3; matrix products, arithmetic and copies ran while one was open for 19% -> 21% of each run, Pallas kernels for 0% -> 0%
where the time goes in v5:
time: 131 us; the launch traced here: 129 us
  starting transfers between devices  48.2 us (37%)
  waiting for transfers between devices  28.8 us (22%)
  blocking collectives  21.4 us (16%)
  matrix products  12.6 us (10%)
  local copies, waits for them, and re-layouts  8.98 us (7%)
  other arithmetic  8.3 us (6%)
    ppermute x12, starting transfers between devices, swap_with(): return lax.ppermute(value, axis, [(i, i ^ mask) for i in range(count)])  34.8 us
    all_to_all x1, blocking collectives, on_device(): activated = lax.all_to_all(act_t, 'feat', 0, 1, tiled=True)  21.4 us
    all_to_all x1, waiting for transfers between devices, on_device(): agg_t = lax.all_to_all(aggregated, 'feat', 1, 0, tiled=True)  14.8 us
    ppermute x12, waiting for transfers between devices, swap_with(): return lax.ppermute(value, axis, [(i, i ^ mask) for i in range(count)])  13.9 us
    dot_general x8, matrix products, add_source(): jnp.einsum('sfj,sji->fsi', picked, tiles_part, preferred_element_type=jnp...  7.96 us
    all_to_all x1, starting transfers between devices, on_device(): lax.all_to_all(tile_col.reshape(cycle_len, slot_total), 'row', 0, 0, tile...  7.47 us
    all_to_all x1, starting transfers between devices, on_device(): agg_t = lax.all_to_all(aggregated, 'feat', 1, 0, tiled=True)  5.92 us
    gather x3, other arithmetic, on_device(): live_all = tile_ids % slot_total < counts_here[tile_ids // slot_total]  5.01 us
  transfers between devices with their start and end apart: 14, of which 3 were waited for; matrix products, arithmetic and copies ran while one was open for 21% of the time, Pallas kernels for 0%

profile of v5, /device:TPU:1, one launch (start us, length us, event | category | flops | bytes accessed | tf_op | source)
XLA Modules:
  0.0 128.8 jit_solution(5140361324197987835)
XLA Ops:
  0.0 1.4 %all_to_all.34 = s32[8,1,32]{2,1,0:T(1,128)} reshape(s32[256]{0:T(256)} %param.10) | data formatting | bytes 2048 | tf_op jit(solution)/shard_map/all_to_all | solution.py:40
  1.4 7.5 %all-to-all-start = ((s32[8,1,32]{2,1,0:T(1,128)}), s32[8,1,32]{2,1,0:T(1,128)S(1)}, u32[]{:S(2)}, u32[]{:S(2)}) async-start(s32[8,1,32]{2,1,0:T(1,128)} %all_to_all.34), calls=%async_computation | async-start | bytes 8192 | tf_op jit(solution)/shard_map/all_to_all | solution.py:40
  10.2 1.6 %fusion.63 = (s32[1,1]{1,0:T(1,128)}, s32[1,1]{1,0:T(1,128)}, s32[1,1]{1,0:T(1,128)}, s32[1,1]{1,0:T(1,128)}, s32[1,1]{1,0:T(1,128)}, /*index=5*/s32[1,1]{1,0:T(1,128)}, s32[1,1]{1,0:T(1,128)}, s32[1,1]{1,0:T(1,128)}) fusion(s32[1,8]{1,0:T(1,128)} %param.11), kind=kLoop, calls=%fused_computation.127 | loop fusion | bytes 64 | tf_op jit(solution)/shard_map/gather | solution.py:44
  11.8 4.3 %compare_select_fusion.2 = s32[256,1]{0,1:T(1,128)S(1)} fusion(s32[]{:T(128)} %bitcast.15, s32[]{:T(128)} %bitcast.16, s32[]{:T(128)} %bitcast.17, s32[]{:T(128)} %bitcast.18, s32[]{:T(128)} %bitcast.19, s32[]{:T(128)} %bitcast.21, s32[]{:T(128)} %bitcast.20), kind=kLoop, calls=%fused_computation.105 | loop fusion | flops 5888 | bytes 1052 | tf_op jit(solution)/shard_map/gather | solution.py:44
  18.4 1.7 %convolution_bitcast_fusion.7 = bf16[32,32,128]{2,0,1:T(8,128)(2,1)S(1)} fusion(bf16[256,128,128]{2,1,0:T(8,128)(2,1)} %param.8, s32[]{:T(128)S(6)} %select_n.225, bf16[32,32,128]{2,1,0:T(8,128)(2,1)S(1)} %gather_fusion, pred[32]{0:T(512)(128)(4,1)S(1)} %get-tuple-element.7), kind=kOutput, calls=%fused_computation.23 | convolution fusion | flops 33685504 | bytes 1572900 | tf_op jit(solution)/shard_map/sfj,sji->fsi/dot_general | solution.py:52
  20.1 1.4 %fusion.18 = f32[64,32,128]{2,0,1:T(8,128)} fusion(bf16[32,32,128]{2,0,1:T(8,128)(2,1)S(1)} %convolution_bitcast_fusion.7, pred[8,32,64]{2,1,0:T(32,128)(4,1)S(1)} %fusion.23, s32[]{:T(128)S(6)} %select_n.224), kind=kOutput, calls=%fused_computation.44 | convolution fusion | flops 16777216 | bytes 1314820 | tf_op jit(solution)/shard_map/fsi,sr->fri/dot_general | solution.py:53
  22.3 1.0 gather_fusion.2
  23.7 7.0 %collective-permute-start.1 = (bf16[2,32,1024]{2,1,0:T(8,128)(2,1)S(1)}, bf16[2,32,1024]{2,1,0:T(8,128)(2,1)S(1)}, u32[]{:S(2)}, u32[]{:S(2)}) collective-permute-start(bf16[2,32,1024]{2,1,0:T(8,128)(2,1)S(1)} %maximum_bitcast_fusion), channel_id=1, source_target_pairs={{0,8},{1,9},{2,10},{3,11},{4,12},{5,13},{6,14},{7,15},{8,0},{9,1},... | collective-permute-start | bytes 393224 | tf_op jit(solution)/shard_map/ppermute | solution.py:9
  31.0 1.6 %collective-permute-start.4 = (bf16[32,32,128]{2,1,0:T(8,128)(2,1)S(1)}, bf16[32,32,128]{2,1,0:T(8,128)(2,1)S(1)}, u32[]{:S(2)}, u32[]{:S(2)}) collective-permute-start(bf16[32,32,128]{2,1,0:T(8,128)(2,1)S(1)} %get-tuple-element.17), channel_id=1, source_target_pairs={{0,32},{32,0},{64,96},{96,64},{128,160},{160,128},{192,224},{224,1... | collective-permute-start | bytes 786440 | tf_op jit(solution)/shard_map/ppermute | solution.py:9
  32.5 2.4 %collective-permute-start.5 = (bf16[32,32,128]{2,1,0:T(8,128)(2,1)S(1)}, bf16[32,32,128]{2,1,0:T(8,128)(2,1)S(1)}, u32[]{:S(2)}, u32[]{:S(2)}) collective-permute-start(bf16[32,32,128]{2,1,0:T(8,128)(2,1)S(1)} %get-tuple-element.16), channel_id=1, source_target_pairs={{0,64},{32,96},{64,0},{96,32},{128,192},{160,224},{192,128},{224,1... | collective-permute-start | bytes 786440 | tf_op jit(solution)/shard_map/ppermute | solution.py:9
  35.0 3.5 %collective-permute-start.7 = (bf16[32,32,128]{2,1,0:T(8,128)(2,1)S(1)}, bf16[32,32,128]{2,1,0:T(8,128)(2,1)S(1)}, u32[]{:S(2)}, u32[]{:S(2)}) collective-permute-start(bf16[32,32,128]{2,1,0:T(8,128)(2,1)S(1)} %get-tuple-element.14), channel_id=1, source_target_pairs={{0,128},{32,160},{64,192},{96,224},{128,0},{160,32},{192,64},{224,... | collective-permute-start | bytes 786440 | tf_op jit(solution)/shard_map/ppermute | solution.py:9
  38.6 6.1 %collective-permute-start.9 = (bf16[32,32,128]{2,1,0:T(8,128)(2,1)S(1)}, bf16[32,32,128]{2,1,0:T(8,128)(2,1)S(1)}, u32[]{:S(2)}, u32[]{:S(2)}) collective-permute-start(bf16[32,32,128]{2,1,0:T(8,128)(2,1)S(1)} %get-tuple-element.12), channel_id=1, source_target_pairs={{0,192},{32,224},{64,128},{96,160},{128,64},{160,96},{192,0},{224,... | collective-permute-start | bytes 786440 | tf_op jit(solution)/shard_map/ppermute | solution.py:9
  44.6 1.6 %convolution_bitcast_fusion.6 = bf16[32,32,128]{2,0,1:T(8,128)(2,1)S(1)} fusion(bf16[32,32,128]{2,1,0:T(8,128)(2,1)S(1)} %collective-permute-done.4, bf16[256,128,128]{2,1,0:T(8,128)(2,1)} %param.8, s32[]{:T(128)S(6)} %select_n.229), kind=kOutput, calls=%fused_computation.22 | convolution fusion | flops 33554432 | bytes 1572868 | tf_op jit(solution)/shard_map/sfj,sji->fsi/dot_general | solution.py:52
  46.3 3.6 %collective-permute-start.10 = (bf16[32,32,128]{2,1,0:T(8,128)(2,1)S(1)}, bf16[32,32,128]{2,1,0:T(8,128)(2,1)S(1)}, u32[]{:S(2)}, u32[]{:S(2)}) collective-permute-start(bf16[32,32,128]{2,1,0:T(8,128)(2,1)S(1)} %get-tuple-element.11), channel_id=1, source_target_pairs={{0,224},{32,192},{64,160},{96,128},{128,96},{160,64},{192,32},{224... | collective-permute-start | bytes 786440 | tf_op jit(solution)/shard_map/ppermute | solution.py:9
  49.8 1.6 %convolution_bitcast_fusion.5 = bf16[32,32,128]{2,0,1:T(8,128)(2,1)S(1)} fusion(bf16[32,32,128]{2,1,0:T(8,128)(2,1)S(1)} %collective-permute-done.5, bf16[256,128,128]{2,1,0:T(8,128)(2,1)} %param.8, s32[]{:T(128)S(6)} %select_n.239), kind=kOutput, calls=%fused_computation.21 | convolution fusion | flops 33554432 | bytes 1572868 | tf_op jit(solution)/shard_map/sfj,sji->fsi/dot_general | solution.py:52
  52.3 1.6 %convolution_bitcast_fusion.4 = bf16[32,32,128]{2,0,1:T(8,128)(2,1)S(1)} fusion(bf16[32,32,128]{2,1,0:T(8,128)(2,1)S(1)} %collective-permute-done.6, bf16[256,128,128]{2,1,0:T(8,128)(2,1)} %param.8, s32[]{:T(128)S(6)} %select_n.241), kind=kOutput, calls=%fused_computation.20 | convolution fusion | flops 33554432 | bytes 1572868 | tf_op jit(solution)/shard_map/sfj,sji->fsi/dot_general | solution.py:52
  56.6 4.2 %collective-permute-done.2 = bf16[4,32,1024]{2,1,0:T(8,128)(2,1)S(1)} collective-permute-done((bf16[4,32,1024]{2,1,0:T(8,128)(2,1)S(1)}, bf16[4,32,1024]{2,1,0:T(8,128)(2,1)S(1)}, u32[]{:S(2)}, u32[]{:S(2)}) %collective-permute-start.2) | collective-permute-done | bytes 262176 | tf_op jit(solution)/shard_map/ppermute | solution.py:9
  62.4 9.7 %collective-permute-done.3 = bf16[8,32,1024]{2,1,0:T(8,128)(2,1)S(1)} collective-permute-done((bf16[8,32,1024]{2,1,0:T(8,128)(2,1)S(1)}, bf16[8,32,1024]{2,1,0:T(8,128)(2,1)S(1)}, u32[]{:S(2)}, u32[]{:S(2)}) %collective-permute-start.3) | collective-permute-done | bytes 524320 | tf_op jit(solution)/shard_map/ppermute | solution.py:9
  72.4 9.6 %collective-permute-start.11 = (bf16[16,32,1024]{2,1,0:T(8,128)(2,1)S(1)}, bf16[16,32,1024]{2,1,0:T(8,128)(2,1)}, u32[]{:S(2)}, u32[]{:S(2)}) collective-permute-start(bf16[16,32,1024]{2,1,0:T(8,128)(2,1)S(1)} %bitcast.127), channel_id=1, source_target_pairs={{0,1},{1,0},{2,3},{3,2},{4,5},{5,4},{6,7},{7,6},{8,9},{9,8},{10,11... | collective-permute-start | bytes 3145736 | tf_op jit(solution)/shard_map/ppermute | solution.py:9
  82.2 1.1 copy.58
  83.3 5.9 %all-to-all-start.1 = ((bf16[32,32,256]{2,0,1:T(8,128)(2,1)}), bf16[32,32,256]{2,0,1:T(8,128)(2,1)S(1)}, u32[]{:S(2)}, u32[]{:S(2)}) async-start(bf16[32,32,256]{2,0,1:T(8,128)(2,1)} %copy.58), calls=%async_computation.1 | async-start | bytes 1048576 | tf_op jit(solution)/shard_map/all_to_all | solution.py:69
  89.3 1.4 %select_bitcast_fusion.1 = (bf16[16,1,32,1024]{3,2,0,1:T(8,128)(2,1)S(1)}, bf16[16,1,32,1024]{3,2,0,1:T(8,128)(2,1)S(1)}) fusion(bf16[16,32,1024]{2,1,0:T(8,128)(2,1)S(1)} %bitcast.128, bf16[16,32,1024]{2,1,0:T(8,128)(2,1)} %collective-permute-done.11, pred[]{:T(512)S(6)} %eq.33), kind=kLoop, calls=%fused_computation.26 | loop fusion | flops 1048576 | bytes 4194305 | tf_op jit(solution)/shard_map/stack | solution.py:24
  91.0 14.8 %all-to-all-done.1 = bf16[32,32,256]{2,0,1:T(8,128)(2,1)S(1)} async-done(((bf16[32,32,256]{2,0,1:T(8,128)(2,1)}), bf16[32,32,256]{2,0,1:T(8,128)(2,1)S(1)}, u32[]{:S(2)}, u32[]{:S(2)}) %all-to-all-start.1) | async-done | bytes 524320 | tf_op jit(solution)/shard_map/all_to_all | solution.py:69
  106.5 21.4 %all_to_all.47 = bf16[32,32,256]{2,1,0:T(8,128)(2,1)S(1)} all-to-all(bf16[32,32,256]{2,1,0:T(8,128)(2,1)S(1)} %bitcast.134), channel_id=1, replica_groups=mesh['row'=8,'feat'=32] {'feat'}, dimensions={0} | all-to-all | bytes 1048576 | tf_op jit(solution)/shard_map/all_to_all | solution.py:72
  (77 shorter events, 12.5 us)
Async XLA Ops:
  0.0 10.1 %copy-start = (bf16[32,8192]{1,0:T(8,128)(2,1)S(1)}, bf16[32,8192]{1,0:T(8,128)(2,1)}, u32[]{:S(2)}) copy-start(bf16[32,8192]{1,0:T(8,128)(2,1)} %param.7) | copy-start | bytes 1572868
  0.0 23.6 %copy-start.2 = (bf16[32,1024]{1,0:T(8,128)(2,1)S(1)}, bf16[32,1024]{1,0:T(8,128)(2,1)}, u32[]{:S(2)}) copy-start(bf16[32,1024]{1,0:T(8,128)(2,1)} %param.12) | copy-start | bytes 196612
  1.4 20.1 %all-to-all-start = ((s32[8,1,32]{2,1,0:T(1,128)}), s32[8,1,32]{2,1,0:T(1,128)S(1)}, u32[]{:S(2)}, u32[]{:S(2)}) async-start(s32[8,1,32]{2,1,0:T(1,128)} %all_to_all.34), calls=%async_computation | async-start | bytes 8192 | tf_op jit(solution)/shard_map/all_to_all | solution.py:40
  8.9 14.7 %collective-permute-start = (bf16[1,32,1024]{2,1,0:T(8,128)(2,1)}, bf16[1,32,1024]{2,1,0:T(8,128)(2,1)S(1)}, u32[]{:S(2)}, u32[]{:S(2)}) collective-permute-start(bf16[1,32,1024]{2,1,0:T(8,128)(2,1)} %bitcast.136), channel_id=1, source_target_pairs={{0,16},{1,17},{2,18},{3,19},{4,20},{5,21},{6,22},{7,23},{8,24},{9,... | collective-permute-start | bytes 196616 | tf_op jit(solution)/shard_map/ppermute | solution.py:9
  23.2 28.2 %copy-start.1 = (f32[64,32,128]{2,0,1:T(8,128)S(1)}, f32[64,32,128]{2,0,1:T(8,128)}, u32[]{:S(2)}) copy-start(f32[64,32,128]{2,0,1:T(8,128)} %fusion.18) | copy-start | bytes 3145732
  23.3 31.0 %slice-start = ((s8[8388608]{0:T(1024)(128)(4,1)}), s8[4194304]{0:T(1024)(128)(4,1)S(1)}, s32[]{:S(2)}) async-start(s8[8388608]{0:T(1024)(128)(4,1)} %bitcast.125), calls=%async_computation.3 | async-start | bytes 8388608
  23.7 14.8 %collective-permute-start.1 = (bf16[2,32,1024]{2,1,0:T(8,128)(2,1)S(1)}, bf16[2,32,1024]{2,1,0:T(8,128)(2,1)S(1)}, u32[]{:S(2)}, u32[]{:S(2)}) collective-permute-start(bf16[2,32,1024]{2,1,0:T(8,128)(2,1)S(1)} %maximum_bitcast_fusion), channel_id=1, source_target_pairs={{0,8},{1,9},{2,10},{3,11},{4,12},{5,13},{6,14},{7,15},{8,0},{9,1},... | collective-permute-start | bytes 393224 | tf_op jit(solution)/shard_map/ppermute | solution.py:9
  31.0 7.6 %collective-permute-start.4 = (bf16[32,32,128]{2,1,0:T(8,128)(2,1)S(1)}, bf16[32,32,128]{2,1,0:T(8,128)(2,1)S(1)}, u32[]{:S(2)}, u32[]{:S(2)}) collective-permute-start(bf16[32,32,128]{2,1,0:T(8,128)(2,1)S(1)} %get-tuple-element.17), channel_id=1, source_target_pairs={{0,32},{32,0},{64,96},{96,64},{128,160},{160,128},{192,224},{224,1... | collective-permute-start | bytes 786440 | tf_op jit(solution)/shard_map/ppermute | solution.py:9
  32.5 13.7 %collective-permute-start.5 = (bf16[32,32,128]{2,1,0:T(8,128)(2,1)S(1)}, bf16[32,32,128]{2,1,0:T(8,128)(2,1)S(1)}, u32[]{:S(2)}, u32[]{:S(2)}) collective-permute-start(bf16[32,32,128]{2,1,0:T(8,128)(2,1)S(1)} %get-tuple-element.16), channel_id=1, source_target_pairs={{0,64},{32,96},{64,0},{96,32},{128,192},{160,224},{192,128},{224,1... | collective-permute-start | bytes 786440 | tf_op jit(solution)/shard_map/ppermute | solution.py:9
  34.9 16.9 %collective-permute-start.6 = (bf16[32,32,128]{2,1,0:T(8,128)(2,1)S(1)}, bf16[32,32,128]{2,1,0:T(8,128)(2,1)S(1)}, u32[]{:S(2)}, u32[]{:S(2)}) collective-permute-start(bf16[32,32,128]{2,1,0:T(8,128)(2,1)S(1)} %get-tuple-element.15), channel_id=1, source_target_pairs={{0,96},{32,64},{64,32},{96,0},{128,224},{160,192},{192,160},{224,1... | collective-permute-start | bytes 786440 | tf_op jit(solution)/shard_map/ppermute | solution.py:9
  35.0 19.3 %collective-permute-start.7 = (bf16[32,32,128]{2,1,0:T(8,128)(2,1)S(1)}, bf16[32,32,128]{2,1,0:T(8,128)(2,1)S(1)}, u32[]{:S(2)}, u32[]{:S(2)}) collective-permute-start(bf16[32,32,128]{2,1,0:T(8,128)(2,1)S(1)} %get-tuple-element.14), channel_id=1, source_target_pairs={{0,128},{32,160},{64,192},{96,224},{128,0},{160,32},{192,64},{224,... | collective-permute-start | bytes 786440 | tf_op jit(solution)/shard_map/ppermute | solution.py:9
  38.5 16.6 %collective-permute-start.8 = (bf16[32,32,128]{2,1,0:T(8,128)(2,1)S(1)}, bf16[32,32,128]{2,1,0:T(8,128)(2,1)S(1)}, u32[]{:S(2)}, u32[]{:S(2)}) collective-permute-start(bf16[32,32,128]{2,1,0:T(8,128)(2,1)S(1)} %get-tuple-element.13), channel_id=1, source_target_pairs={{0,160},{32,128},{64,224},{96,192},{128,32},{160,0},{192,96},{224,... | collective-permute-start | bytes 786440 | tf_op jit(solution)/shard_map/ppermute | solution.py:9
  38.6 15.7 %slice-start.1 = ((s8[8388608]{0:T(1024)(128)(4,1)}), s8[4194304]{0:T(1024)(128)(4,1)S(1)}, s32[]{:S(2)}) async-start(s8[8388608]{0:T(1024)(128)(4,1)} %bitcast.125), calls=%async_computation.4 | async-start | bytes 8388608
  38.6 17.3 %collective-permute-start.9 = (bf16[32,32,128]{2,1,0:T(8,128)(2,1)S(1)}, bf16[32,32,128]{2,1,0:T(8,128)(2,1)S(1)}, u32[]{:S(2)}, u32[]{:S(2)}) collective-permute-start(bf16[32,32,128]{2,1,0:T(8,128)(2,1)S(1)} %get-tuple-element.12), channel_id=1, source_target_pairs={{0,192},{32,224},{64,128},{96,160},{128,64},{160,96},{192,0},{224,... | collective-permute-start | bytes 786440 | tf_op jit(solution)/shard_map/ppermute | solution.py:9
  46.3 15.4 %collective-permute-start.10 = (bf16[32,32,128]{2,1,0:T(8,128)(2,1)S(1)}, bf16[32,32,128]{2,1,0:T(8,128)(2,1)S(1)}, u32[]{:S(2)}, u32[]{:S(2)}) collective-permute-start(bf16[32,32,128]{2,1,0:T(8,128)(2,1)S(1)} %get-tuple-element.11), channel_id=1, source_target_pairs={{0,224},{32,192},{64,160},{96,128},{128,96},{160,64},{192,32},{224... | collective-permute-start | bytes 786440 | tf_op jit(solution)/shard_map/ppermute | solution.py:9
  51.8 9.0 %collective-permute-start.2 = (bf16[4,32,1024]{2,1,0:T(8,128)(2,1)S(1)}, bf16[4,32,1024]{2,1,0:T(8,128)(2,1)S(1)}, u32[]{:S(2)}, u32[]{:S(2)}) collective-permute-start(bf16[4,32,1024]{2,1,0:T(8,128)(2,1)S(1)} %bitcast.132), channel_id=1, source_target_pairs={{0,4},{1,5},{2,6},{3,7},{4,0},{5,1},{6,2},{7,3},{8,12},{9,13},{10,... | collective-permute-start | bytes 786440 | tf_op jit(solution)/shard_map/ppermute | solution.py:9
  61.0 11.1 %collective-permute-start.3 = (bf16[8,32,1024]{2,1,0:T(8,128)(2,1)S(1)}, bf16[8,32,1024]{2,1,0:T(8,128)(2,1)S(1)}, u32[]{:S(2)}, u32[]{:S(2)}) collective-permute-start(bf16[8,32,1024]{2,1,0:T(8,128)(2,1)S(1)} %bitcast.129), channel_id=1, source_target_pairs={{0,2},{1,3},{2,0},{3,1},{4,6},{5,7},{6,4},{7,5},{8,10},{9,11},{10,... | collective-permute-start | bytes 1572872 | tf_op jit(solution)/shard_map/ppermute | solution.py:9
  72.4 33.4 %copy-start.3 = (f32[1024]{0:T(1024)S(1)}, f32[1024]{0:T(1024)}, u32[]{:S(2)}) copy-start(f32[1024]{0:T(1024)} %param.13) | copy-start | bytes 12292
  72.4 16.8 %collective-permute-start.11 = (bf16[16,32,1024]{2,1,0:T(8,128)(2,1)S(1)}, bf16[16,32,1024]{2,1,0:T(8,128)(2,1)}, u32[]{:S(2)}, u32[]{:S(2)}) collective-permute-start(bf16[16,32,1024]{2,1,0:T(8,128)(2,1)S(1)} %bitcast.127), channel_id=1, source_target_pairs={{0,1},{1,0},{2,3},{3,2},{4,5},{5,4},{6,7},{7,6},{8,9},{9,8},{10,11... | collective-permute-start | bytes 3145736 | tf_op jit(solution)/shard_map/ppermute | solution.py:9
  83.3 22.5 %all-to-all-start.1 = ((bf16[32,32,256]{2,0,1:T(8,128)(2,1)}), bf16[32,32,256]{2,0,1:T(8,128)(2,1)S(1)}, u32[]{:S(2)}, u32[]{:S(2)}) async-start(bf16[32,32,256]{2,0,1:T(8,128)(2,1)} %copy.58), calls=%async_computation.1 | async-start | bytes 1048576 | tf_op jit(solution)/shard_map/all_to_all | solution.py:69

commit v6 on v2

--- a/solution.py
+++ b/solution.py
@@ -13,14 +13,20 @@
     feat_count = lax.axis_size("feat")
     me = lax.axis_index("feat")
     bits = feat_count.bit_length() - 1
-    order = [bits - 1] + list(range(bits - 2, 0, -1)) + [0]
+    order = list(range(bits - 2, 0, -1)) + [bits - 1, 0]
     held = weight.reshape(1, -1, weight.shape[1])
+    done = []
     for bit in order:
         theirs = swap_with(held, "feat", 1 << bit)
         mine_low = ((me >> bit) & 1) == 0
         low = jnp.where(mine_low, held, theirs)
         high = jnp.where(mine_low, theirs, held)
-        held = jnp.stack([low, high], axis=1).reshape(-1, *held.shape[1:])
+        above = 2 ** sum(1 for b in done if b > bit)
+        pair = jnp.stack(
+            [low.reshape(above, -1, *held.shape[1:]), high.reshape(above, -1, *held.shape[1:])], axis=1
+        )
+        held = pair.reshape(-1, *held.shape[1:])
+        done.append(bit)
     return held.reshape(-1, weight.shape[1])
 
 

time: 132 us -> 129 us (0.977)
  the two profiles are of different devices: /device:TPU:1 before, /device:TPU:24 now
where the time goes in v6:
time: 129 us
  starting transfers between devices  49.3 us (38%)
  waiting for transfers between devices  29.1 us (23%)
  blocking collectives  21.4 us (17%)
  matrix products  11.4 us (9%)
  local copies, waits for them, and re-layouts  8.73 us (7%)
  other arithmetic  8.31 us (6%)
    ppermute x12, starting transfers between devices, swap_with(): return lax.ppermute(value, axis, [(i, i ^ mask) for i in range(count)])  38.3 us
    all_to_all x1, blocking collectives, on_device(): activated = lax.all_to_all(act_t, 'feat', 0, 1, tiled=True)  21.4 us
    all_to_all x1, waiting for transfers between devices, on_device(): agg_t = lax.all_to_all(aggregated, 'feat', 1, 0, tiled=True)  16.8 us
    ppermute x12, waiting for transfers between devices, swap_with(): return lax.ppermute(value, axis, [(i, i ^ mask) for i in range(count)])  12.3 us
    all_to_all x1, starting transfers between devices, on_device(): lax.all_to_all(tile_col.reshape(cycle_len, slot_total), 'row', 0, 0, tile...  7.15 us
    dot_general x8, matrix products, add_source(): jnp.einsum('sfj,sji->fsi', picked, tiles_part, preferred_element_type=jnp...  6.74 us
    gather x3, other arithmetic, on_device(): live_all = tile_ids % slot_total < counts_here[tile_ids // slot_total]  5.01 us
    dot_general x8, matrix products, add_source(): return running + jnp.einsum('fsi,sr->fri', product, onehot)  3.96 us
  transfers between devices with their start and end apart: 14, of which 3 were waited for; matrix products, arithmetic and copies ran while one was open for 20% of the time, Pallas kernels for 0%

profile of v6, /device:TPU:24, one launch (start us, length us, event | category | flops | bytes accessed | tf_op | source)
XLA Modules:
  0.0 128.8 jit_solution(16215755681192799000)
XLA Ops:
  0.0 1.4 %all_to_all.34 = s32[8,1,32]{2,1,0:T(1,128)} reshape(s32[256]{0:T(256)} %param.10) | data formatting | bytes 2048 | tf_op jit(solution)/shard_map/all_to_all | solution.py:44
  1.4 7.1 %all-to-all-start = ((s32[8,1,32]{2,1,0:T(1,128)}), s32[8,1,32]{2,1,0:T(1,128)S(1)}, u32[]{:S(2)}, u32[]{:S(2)}) async-start(s32[8,1,32]{2,1,0:T(1,128)} %all_to_all.34), calls=%async_computation | async-start | bytes 8192 | tf_op jit(solution)/shard_map/all_to_all | solution.py:44
  8.6 7.2 %collective-permute-start = (bf16[1,32,1024]{2,1,0:T(8,128)(2,1)}, bf16[1,32,1024]{2,1,0:T(8,128)(2,1)S(1)}, u32[]{:S(2)}, u32[]{:S(2)}) collective-permute-start(bf16[1,32,1024]{2,1,0:T(8,128)(2,1)} %bitcast.141), channel_id=1, source_target_pairs={{0,8},{1,9},{2,10},{3,11},{4,12},{5,13},{6,14},{7,15},{8,0},{9,1},... | collective-permute-start | bytes 196616 | tf_op jit(solution)/shard_map/ppermute | solution.py:9
  16.8 1.6 %fusion.64 = (s32[1,1]{1,0:T(1,128)}, s32[1,1]{1,0:T(1,128)}, s32[1,1]{1,0:T(1,128)}, s32[1,1]{1,0:T(1,128)}, s32[1,1]{1,0:T(1,128)}, /*index=5*/s32[1,1]{1,0:T(1,128)}, s32[1,1]{1,0:T(1,128)}, s32[1,1]{1,0:T(1,128)}) fusion(s32[1,8]{1,0:T(1,128)} %param.11), kind=kLoop, calls=%fused_computation.128 | loop fusion | bytes 64 | tf_op jit(solution)/shard_map/gather | solution.py:48
  18.4 4.3 %compare_select_fusion.2 = s32[256,1]{0,1:T(1,128)S(1)} fusion(s32[]{:T(128)} %bitcast.20, s32[]{:T(128)} %bitcast.21, s32[]{:T(128)} %bitcast.22, s32[]{:T(128)} %bitcast.23, s32[]{:T(128)} %bitcast.24, s32[]{:T(128)} %bitcast.26, s32[]{:T(128)} %bitcast.25), kind=kLoop, calls=%fused_computation.106 | loop fusion | flops 5888 | bytes 1052 | tf_op jit(solution)/shard_map/gather | solution.py:48
  25.0 1.7 %convolution_bitcast_fusion.7 = bf16[32,32,128]{2,0,1:T(8,128)(2,1)S(1)} fusion(bf16[256,128,128]{2,1,0:T(8,128)(2,1)} %param.8, s32[]{:T(128)S(6)} %select_n.227, bf16[32,32,128]{2,1,0:T(8,128)(2,1)S(1)} %gather_fusion, pred[32]{0:T(512)(128)(4,1)S(1)} %get-tuple-element.5), kind=kOutput, calls=%fused_computation.24 | convolution fusion | flops 33685504 | bytes 1572900 | tf_op jit(solution)/shard_map/sfj,sji->fsi/dot_general | solution.py:56
  26.7 1.4 %fusion.19 = f32[64,32,128]{2,0,1:T(8,128)} fusion(bf16[32,32,128]{2,0,1:T(8,128)(2,1)S(1)} %convolution_bitcast_fusion.7, pred[8,32,64]{2,1,0:T(32,128)(4,1)S(1)} %fusion.24, s32[]{:T(128)S(6)} %select_n.226), kind=kOutput, calls=%fused_computation.45 | convolution fusion | flops 16777216 | bytes 1314820 | tf_op jit(solution)/shard_map/fsi,sr->fri/dot_general | solution.py:57
  28.8 1.0 gather_fusion.2
  30.2 1.6 %collective-permute-start.1 = (bf16[2,32,1024]{2,1,0:T(8,128)(2,1)S(1)}, bf16[2,32,1024]{2,1,0:T(8,128)(2,1)S(1)}, u32[]{:S(2)}, u32[]{:S(2)}) collective-permute-start(bf16[2,32,1024]{2,1,0:T(8,128)(2,1)S(1)} %maximum_bitcast_fusion), channel_id=1, source_target_pairs={{0,4},{1,5},{2,6},{3,7},{4,0},{5,1},{6,2},{7,3},{8,12},{9,13},{10,... | collective-permute-start | bytes 393224 | tf_op jit(solution)/shard_map/ppermute | solution.py:9
  32.1 0.9 collective-permute-start.5
  33.8 3.1 %collective-permute-start.7 = (bf16[32,32,128]{2,1,0:T(8,128)(2,1)S(1)}, bf16[32,32,128]{2,1,0:T(8,128)(2,1)S(1)}, u32[]{:S(2)}, u32[]{:S(2)}) collective-permute-start(bf16[32,32,128]{2,1,0:T(8,128)(2,1)S(1)} %get-tuple-element.13), channel_id=1, source_target_pairs={{0,96},{32,64},{64,32},{96,0},{128,224},{160,192},{192,160},{224,1... | collective-permute-start | bytes 786440 | tf_op jit(solution)/shard_map/ppermute | solution.py:9
  36.9 3.0 %collective-permute-start.8 = (bf16[32,32,128]{2,1,0:T(8,128)(2,1)S(1)}, bf16[32,32,128]{2,1,0:T(8,128)(2,1)S(1)}, u32[]{:S(2)}, u32[]{:S(2)}) collective-permute-start(bf16[32,32,128]{2,1,0:T(8,128)(2,1)S(1)} %get-tuple-element.12), channel_id=1, source_target_pairs={{0,128},{32,160},{64,192},{96,224},{128,0},{160,32},{192,64},{224,... | collective-permute-start | bytes 786440 | tf_op jit(solution)/shard_map/ppermute | solution.py:9
  39.9 1.8 %collective-permute-start.9 = (bf16[32,32,128]{2,1,0:T(8,128)(2,1)S(1)}, bf16[32,32,128]{2,1,0:T(8,128)(2,1)S(1)}, u32[]{:S(2)}, u32[]{:S(2)}) collective-permute-start(bf16[32,32,128]{2,1,0:T(8,128)(2,1)S(1)} %get-tuple-element.11), channel_id=1, source_target_pairs={{0,160},{32,128},{64,224},{96,192},{128,32},{160,0},{192,96},{224,... | collective-permute-start | bytes 786440 | tf_op jit(solution)/shard_map/ppermute | solution.py:9
  41.8 3.5 %collective-permute-start.10 = (bf16[32,32,128]{2,1,0:T(8,128)(2,1)S(1)}, bf16[32,32,128]{2,1,0:T(8,128)(2,1)S(1)}, u32[]{:S(2)}, u32[]{:S(2)}) collective-permute-start(bf16[32,32,128]{2,1,0:T(8,128)(2,1)S(1)} %get-tuple-element.10), channel_id=1, source_target_pairs={{0,192},{32,224},{64,128},{96,160},{128,64},{160,96},{192,0},{224,... | collective-permute-start | bytes 786440 | tf_op jit(solution)/shard_map/ppermute | solution.py:9
  45.2 1.6 %convolution_bitcast_fusion.6 = bf16[32,32,128]{2,0,1:T(8,128)(2,1)S(1)} fusion(bf16[32,32,128]{2,1,0:T(8,128)(2,1)S(1)} %collective-permute-done.5, bf16[256,128,128]{2,1,0:T(8,128)(2,1)} %param.8, s32[]{:T(128)S(6)} %select_n.231), kind=kOutput, calls=%fused_computation.23 | convolution fusion | flops 33554432 | bytes 1572868 | tf_op jit(solution)/shard_map/sfj,sji->fsi/dot_general | solution.py:56
  47.2 15.5 %collective-permute-start.11 = (bf16[32,32,128]{2,1,0:T(8,128)(2,1)S(1)}, bf16[32,32,128]{2,1,0:T(8,128)(2,1)S(1)}, u32[]{:S(2)}, u32[]{:S(2)}) collective-permute-start(bf16[32,32,128]{2,1,0:T(8,128)(2,1)S(1)} %get-tuple-element.9), channel_id=1, source_target_pairs={{0,224},{32,192},{64,160},{96,128},{128,96},{160,64},{192,32},{224... | collective-permute-start | bytes 786440 | tf_op jit(solution)/shard_map/ppermute | solution.py:9
  62.7 1.6 %convolution_bitcast_fusion.5 = bf16[32,32,128]{2,0,1:T(8,128)(2,1)S(1)} fusion(bf16[32,32,128]{2,1,0:T(8,128)(2,1)S(1)} %collective-permute-done.6, bf16[256,128,128]{2,1,0:T(8,128)(2,1)} %param.8, s32[]{:T(128)S(6)} %select_n.241), kind=kOutput, calls=%fused_computation.22 | convolution fusion | flops 33554432 | bytes 1572868 | tf_op jit(solution)/shard_map/sfj,sji->fsi/dot_general | solution.py:56
  66.4 4.8 %collective-permute-done.2 = bf16[4,32,1024]{2,1,0:T(8,128)(2,1)S(1)} collective-permute-done((bf16[4,32,1024]{2,1,0:T(8,128)(2,1)S(1)}, bf16[4,32,1024]{2,1,0:T(8,128)(2,1)S(1)}, u32[]{:S(2)}, u32[]{:S(2)}) %collective-permute-start.2) | collective-permute-done | bytes 262176 | tf_op jit(solution)/shard_map/ppermute | solution.py:9
  73.3 7.4 %collective-permute-done.3 = bf16[8,32,1024]{2,1,0:T(8,128)(2,1)S(1)} collective-permute-done((bf16[8,32,1024]{2,1,0:T(8,128)(2,1)S(1)}, bf16[8,32,1024]{2,1,0:T(8,128)(2,1)S(1)}, u32[]{:S(2)}, u32[]{:S(2)}) %collective-permute-start.3) | collective-permute-done | bytes 524320 | tf_op jit(solution)/shard_map/ppermute | solution.py:9
  82.4 1.1 copy.43
  83.5 3.9 %all-to-all-start.1 = ((bf16[32,32,256]{2,0,1:T(8,128)(2,1)}), bf16[32,32,256]{2,0,1:T(8,128)(2,1)S(1)}, u32[]{:S(2)}, u32[]{:S(2)}) async-start(bf16[32,32,256]{2,0,1:T(8,128)(2,1)} %copy.43), calls=%async_computation.1 | async-start | bytes 1048576 | tf_op jit(solution)/shard_map/all_to_all | solution.py:71
  87.4 1.4 %select_bitcast_fusion.1 = (bf16[16,1,1,32,1024]{4,3,1,0,2:T(8,128)(2,1)S(1)}, bf16[16,1,1,32,1024]{4,3,1,0,2:T(8,128)(2,1)S(1)}) fusion(bf16[16,32,1024]{2,1,0:T(8,128)(2,1)} %collective-permute-done.4, pred[]{:T(512)S(6)} %eq.33, bf16[1,2,8,32,1024]{4,3,2,1,0:T(8,128)(2,1)S(1)} %pad_maximum_fusion.1), kind=kLoop, calls=%fused_computation.35 | loop fusion | flops 1048576 | bytes 4194305 | tf_op jit(solution)/shard_map/stack;reshape | solution.py:25
  89.0 16.8 %all-to-all-done.1 = bf16[32,32,256]{2,0,1:T(8,128)(2,1)S(1)} async-done(((bf16[32,32,256]{2,0,1:T(8,128)(2,1)}), bf16[32,32,256]{2,0,1:T(8,128)(2,1)S(1)}, u32[]{:S(2)}, u32[]{:S(2)}) %all-to-all-start.1) | async-done | bytes 524320 | tf_op jit(solution)/shard_map/all_to_all | solution.py:71
  106.5 21.4 %all_to_all.47 = bf16[32,32,256]{2,1,0:T(8,128)(2,1)S(1)} all-to-all(bf16[32,32,256]{2,1,0:T(8,128)(2,1)S(1)} %bitcast.139), channel_id=1, replica_groups=mesh['row'=8,'feat'=32] {'feat'}, dimensions={0} | all-to-all | bytes 1048576 | tf_op jit(solution)/shard_map/all_to_all | solution.py:74
  (75 shorter events, 13.2 us)
Async XLA Ops:
  0.0 16.7 %copy-start = (bf16[32,8192]{1,0:T(8,128)(2,1)S(1)}, bf16[32,8192]{1,0:T(8,128)(2,1)}, u32[]{:S(2)}) copy-start(bf16[32,8192]{1,0:T(8,128)(2,1)} %param.7) | copy-start | bytes 1572868
  0.0 30.2 %copy-start.2 = (bf16[32,1024]{1,0:T(8,128)(2,1)S(1)}, bf16[32,1024]{1,0:T(8,128)(2,1)}, u32[]{:S(2)}) copy-start(bf16[32,1024]{1,0:T(8,128)(2,1)} %param.12) | copy-start | bytes 196612
  1.4 26.6 %all-to-all-start = ((s32[8,1,32]{2,1,0:T(1,128)}), s32[8,1,32]{2,1,0:T(1,128)S(1)}, u32[]{:S(2)}, u32[]{:S(2)}) async-start(s32[8,1,32]{2,1,0:T(1,128)} %all_to_all.34), calls=%async_computation | async-start | bytes 8192 | tf_op jit(solution)/shard_map/all_to_all | solution.py:44
  8.6 21.6 %collective-permute-start = (bf16[1,32,1024]{2,1,0:T(8,128)(2,1)}, bf16[1,32,1024]{2,1,0:T(8,128)(2,1)S(1)}, u32[]{:S(2)}, u32[]{:S(2)}) collective-permute-start(bf16[1,32,1024]{2,1,0:T(8,128)(2,1)} %bitcast.141), channel_id=1, source_target_pairs={{0,8},{1,9},{2,10},{3,11},{4,12},{5,13},{6,14},{7,15},{8,0},{9,1},... | collective-permute-start | bytes 196616 | tf_op jit(solution)/shard_map/ppermute | solution.py:9
  29.8 17.0 %copy-start.1 = (f32[64,32,128]{2,0,1:T(8,128)S(1)}, f32[64,32,128]{2,0,1:T(8,128)}, u32[]{:S(2)}) copy-start(f32[64,32,128]{2,0,1:T(8,128)} %fusion.19) | copy-start | bytes 3145732
  29.8 35.0 %slice-start = ((s8[8388608]{0:T(1024)(128)(4,1)}), s8[4194304]{0:T(1024)(128)(4,1)S(1)}, s32[]{:S(2)}) async-start(s8[8388608]{0:T(1024)(128)(4,1)} %bitcast.131), calls=%async_computation.3 | async-start | bytes 8388608
  30.2 9.6 %collective-permute-start.1 = (bf16[2,32,1024]{2,1,0:T(8,128)(2,1)S(1)}, bf16[2,32,1024]{2,1,0:T(8,128)(2,1)S(1)}, u32[]{:S(2)}, u32[]{:S(2)}) collective-permute-start(bf16[2,32,1024]{2,1,0:T(8,128)(2,1)S(1)} %maximum_bitcast_fusion), channel_id=1, source_target_pairs={{0,4},{1,5},{2,6},{3,7},{4,0},{5,1},{6,2},{7,3},{8,12},{9,13},{10,... | collective-permute-start | bytes 393224 | tf_op jit(solution)/shard_map/ppermute | solution.py:9
  32.1 9.6 %collective-permute-start.5 = (bf16[32,32,128]{2,1,0:T(8,128)(2,1)S(1)}, bf16[32,32,128]{2,1,0:T(8,128)(2,1)S(1)}, u32[]{:S(2)}, u32[]{:S(2)}) collective-permute-start(bf16[32,32,128]{2,1,0:T(8,128)(2,1)S(1)} %get-tuple-element.15), channel_id=1, source_target_pairs={{0,32},{32,0},{64,96},{96,64},{128,160},{160,128},{192,224},{224,1... | collective-permute-start | bytes 786440 | tf_op jit(solution)/shard_map/ppermute | solution.py:9
  33.1 14.2 %collective-permute-start.6 = (bf16[32,32,128]{2,1,0:T(8,128)(2,1)S(1)}, bf16[32,32,128]{2,1,0:T(8,128)(2,1)S(1)}, u32[]{:S(2)}, u32[]{:S(2)}) collective-permute-start(bf16[32,32,128]{2,1,0:T(8,128)(2,1)S(1)} %get-tuple-element.14), channel_id=1, source_target_pairs={{0,64},{32,96},{64,0},{96,32},{128,192},{160,224},{192,128},{224,1... | collective-permute-start | bytes 786440 | tf_op jit(solution)/shard_map/ppermute | solution.py:9
  33.8 30.9 %collective-permute-start.7 = (bf16[32,32,128]{2,1,0:T(8,128)(2,1)S(1)}, bf16[32,32,128]{2,1,0:T(8,128)(2,1)S(1)}, u32[]{:S(2)}, u32[]{:S(2)}) collective-permute-start(bf16[32,32,128]{2,1,0:T(8,128)(2,1)S(1)} %get-tuple-element.13), channel_id=1, source_target_pairs={{0,96},{32,64},{64,32},{96,0},{128,224},{160,192},{192,160},{224,1... | collective-permute-start | bytes 786440 | tf_op jit(solution)/shard_map/ppermute | solution.py:9
  36.9 28.7 %collective-permute-start.8 = (bf16[32,32,128]{2,1,0:T(8,128)(2,1)S(1)}, bf16[32,32,128]{2,1,0:T(8,128)(2,1)S(1)}, u32[]{:S(2)}, u32[]{:S(2)}) collective-permute-start(bf16[32,32,128]{2,1,0:T(8,128)(2,1)S(1)} %get-tuple-element.12), channel_id=1, source_target_pairs={{0,128},{32,160},{64,192},{96,224},{128,0},{160,32},{192,64},{224,... | collective-permute-start | bytes 786440 | tf_op jit(solution)/shard_map/ppermute | solution.py:9
  39.9 32.3 %collective-permute-start.9 = (bf16[32,32,128]{2,1,0:T(8,128)(2,1)S(1)}, bf16[32,32,128]{2,1,0:T(8,128)(2,1)S(1)}, u32[]{:S(2)}, u32[]{:S(2)}) collective-permute-start(bf16[32,32,128]{2,1,0:T(8,128)(2,1)S(1)} %get-tuple-element.11), channel_id=1, source_target_pairs={{0,160},{32,128},{64,224},{96,192},{128,32},{160,0},{192,96},{224,... | collective-permute-start | bytes 786440 | tf_op jit(solution)/shard_map/ppermute | solution.py:9
  41.7 23.1 %slice-start.1 = ((s8[8388608]{0:T(1024)(128)(4,1)}), s8[4194304]{0:T(1024)(128)(4,1)S(1)}, s32[]{:S(2)}) async-start(s8[8388608]{0:T(1024)(128)(4,1)} %bitcast.131), calls=%async_computation.4 | async-start | bytes 8388608
  41.8 30.8 %collective-permute-start.10 = (bf16[32,32,128]{2,1,0:T(8,128)(2,1)S(1)}, bf16[32,32,128]{2,1,0:T(8,128)(2,1)S(1)}, u32[]{:S(2)}, u32[]{:S(2)}) collective-permute-start(bf16[32,32,128]{2,1,0:T(8,128)(2,1)S(1)} %get-tuple-element.10), channel_id=1, source_target_pairs={{0,192},{32,224},{64,128},{96,160},{128,64},{160,96},{192,0},{224,... | collective-permute-start | bytes 786440 | tf_op jit(solution)/shard_map/ppermute | solution.py:9
  47.2 34.2 %collective-permute-start.11 = (bf16[32,32,128]{2,1,0:T(8,128)(2,1)S(1)}, bf16[32,32,128]{2,1,0:T(8,128)(2,1)S(1)}, u32[]{:S(2)}, u32[]{:S(2)}) collective-permute-start(bf16[32,32,128]{2,1,0:T(8,128)(2,1)S(1)} %get-tuple-element.9), channel_id=1, source_target_pairs={{0,224},{32,192},{64,160},{96,128},{128,96},{160,64},{192,32},{224... | collective-permute-start | bytes 786440 | tf_op jit(solution)/shard_map/ppermute | solution.py:9
  64.7 6.5 %collective-permute-start.2 = (bf16[4,32,1024]{2,1,0:T(8,128)(2,1)S(1)}, bf16[4,32,1024]{2,1,0:T(8,128)(2,1)S(1)}, u32[]{:S(2)}, u32[]{:S(2)}) collective-permute-start(bf16[4,32,1024]{2,1,0:T(8,128)(2,1)S(1)} %bitcast.137), channel_id=1, source_target_pairs={{0,2},{1,3},{2,0},{3,1},{4,6},{5,7},{6,4},{7,5},{8,10},{9,11},{10,... | collective-permute-start | bytes 786440 | tf_op jit(solution)/shard_map/ppermute | solution.py:9
  71.3 9.4 %collective-permute-start.3 = (bf16[8,32,1024]{2,1,0:T(8,128)(2,1)S(1)}, bf16[8,32,1024]{2,1,0:T(8,128)(2,1)S(1)}, u32[]{:S(2)}, u32[]{:S(2)}) collective-permute-start(bf16[8,32,1024]{2,1,0:T(8,128)(2,1)S(1)} %bitcast.134), channel_id=1, source_target_pairs={{0,16},{1,17},{2,18},{3,19},{4,20},{5,21},{6,22},{7,23},{8,24},{9,... | collective-permute-start | bytes 1572872 | tf_op jit(solution)/shard_map/ppermute | solution.py:9
  81.0 24.8 %copy-start.3 = (f32[1024]{0:T(1024)S(1)}, f32[1024]{0:T(1024)}, u32[]{:S(2)}) copy-start(f32[1024]{0:T(1024)} %param.13) | copy-start | bytes 12292
  81.0 6.4 %collective-permute-start.4 = (bf16[16,32,1024]{2,1,0:T(8,128)(2,1)S(1)}, bf16[16,32,1024]{2,1,0:T(8,128)(2,1)}, u32[]{:S(2)}, u32[]{:S(2)}) collective-permute-start(bf16[16,32,1024]{2,1,0:T(8,128)(2,1)S(1)} %bitcast.133), channel_id=1, source_target_pairs={{0,1},{1,0},{2,3},{3,2},{4,5},{5,4},{6,7},{7,6},{8,9},{9,8},{10,11... | collective-permute-start | bytes 3145736 | tf_op jit(solution)/shard_map/ppermute | solution.py:9
  83.5 22.3 %all-to-all-start.1 = ((bf16[32,32,256]{2,0,1:T(8,128)(2,1)}), bf16[32,32,256]{2,0,1:T(8,128)(2,1)S(1)}, u32[]{:S(2)}, u32[]{:S(2)}) async-start(bf16[32,32,256]{2,0,1:T(8,128)(2,1)} %copy.43), calls=%async_computation.1 | async-start | bytes 1048576 | tf_op jit(solution)/shard_map/all_to_all | solution.py:71
